TPU v7x, 32 devices: a whole 2x2x4 slice. The times are simulated.
32 devices in a mesh: seq: 8 (over y, x, core), tp: 4 (over z).
Axes of the slice: x: 2, y: 2, z: 4, core: 2. Of those that a mesh axis runs over, the one named last changes fastest.
Arguments:
- projected: bfloat16 [1536, 3, 8192], P('seq', None, 'tp'), may hold values from -6 to 6
- feat_taps: float32 [7, 3, 8192], P(None, None, 'tp'), may hold values from -2.5 to 2.5
- filters: float32 [512, 128], P('tp'), may hold values from -1.5 to 1.5
- out_weight: bfloat16 [8192, 8192], P('tp'), may hold values from -0.09375 to 0.09375
- cotangent: bfloat16 [1536, 8192], P('seq', 'tp'), may hold values from -6 to 6
Outputs:
- output: bfloat16 [1536, 8192], P('seq', 'tp')
- input_grad: bfloat16 [1536, 3, 8192], P('seq', None, 'tp')
All inputs are finite; a program needn't handle non-finite values.
Results may differ from a plain program's by a relative error of at most 0.0095.
Values may be sent and summed in bfloat16 or wider, within the bound.
No kernel may reach another device: no remote copies, remote signals or barrier semaphores. Data moves between devices by JAX's collectives and lax.ppermute only.
A program may use at most 128 MiB of HBM per device.

v0:
```python
import jax
import jax.numpy as jnp
from jax import lax
from jax.experimental import pallas as pl
from jax.experimental.pallas import tpu as pltpu
from jax.sharding import PartitionSpec as P

LANES = 128


def _toeplitz_kernel(base_ref, ext_ref, out_ref):
    gb, span = base_ref.shape
    rows, width = out_ref.shape
    half = rows // 2
    hg = width // gb
    p = ext_ref[...]
    p2 = jnp.concatenate([p[:span], p[half:half + span]], axis=1)
    p_hi = p2.astype(jnp.bfloat16)
    p_lo = (p2 - p_hi.astype(jnp.float32)).astype(jnp.bfloat16)
    lane_group = (lax.broadcasted_iota(jnp.int32, (half, 2 * width), 1) % width) // hg
    acc = jnp.zeros((half, 2 * width), jnp.float32)
    for g in range(gb):
        t = jnp.broadcast_to(base_ref[pl.ds(g, 1), :], (half, span))
        t = pltpu.roll(t, 0, 1, stride=1, stride_axis=0).astype(jnp.bfloat16)
        res = jnp.dot(t, p_hi, preferred_element_type=jnp.float32)
        res = res + jnp.dot(t, p_lo, preferred_element_type=jnp.float32)
        acc = jnp.where(lane_group == g, res, acc)
    out_ref[pl.ds(0, half), :] = acc[:, :width]
    out_ref[pl.ds(half, half), :] = acc[:, width:]


def toeplitz_conv(base, ext, rows):
    groups, span = base.shape
    length, channels = ext.shape
    half = rows // 2
    assert rows % 32 == 0 and half + span <= length and span >= half + LANES - 1
    gb = groups * LANES // channels
    steps = channels // LANES
    flops = 4 * half * span * 2 * LANES * gb * steps
    return pl.pallas_call(
        _toeplitz_kernel,
        grid=(steps,),
        in_specs=[
            pl.BlockSpec((gb, span), lambda i: (i, 0)),
            pl.BlockSpec((length, LANES), lambda i: (0, i)),
        ],
        out_specs=pl.BlockSpec((rows, LANES), lambda i: (0, i)),
        out_shape=jax.ShapeDtypeStruct((rows, channels), jnp.float32),
        cost_estimate=pl.CostEstimate(
            flops=flops, transcendentals=0,
            bytes_accessed=4 * (base.size + ext.size + rows * channels)),
    )(base, ext)


def shift_perm(n, step):
    if step > 0:
        return [(j, j + 1) for j in range(n - 1)]
    return [(j + 1, j) for j in range(n - 1)]


def block(projected, feat_taps, filters, out_weight, cotangent):
    rows = projected.shape[0]
    feat_len = feat_taps.shape[0]
    filt_len = filters.shape[1]
    channels = projected.shape[2]
    n = lax.axis_size("seq")
    fwd = shift_perm(n, 1)
    bwd = shift_perm(n, -1)
    fh = feat_len - 1
    lh = filt_len - 1
    reach = lh + fh
    assert reach <= rows
    ext_len = -(-(rows + reach) // LANES) * LANES
    fwd_rows = rows
    bwd_rows = -(-(rows + fh) // 32) * 32
    span_f = -(-(fwd_rows // 2 + lh) // LANES) * LANES
    span_b = -(-(bwd_rows // 2 + lh) // LANES) * LANES
    base_fwd = jnp.pad(filters[:, ::-1], ((0, 0), (0, span_f - filt_len))).astype(jnp.bfloat16)
    base_bwd = jnp.pad(filters, ((0, 0), (0, span_b - filt_len))).astype(jnp.bfloat16)
    base_fwd = base_fwd.astype(jnp.float32)
    base_bwd = base_bwd.astype(jnp.float32)

    prev_proj = lax.ppermute(projected[rows - fh:], "seq", fwd)
    next_proj = lax.ppermute(projected[:fh], "seq", bwd)
    ext = jnp.concatenate([prev_proj, projected, next_proj], axis=0).astype(jnp.float32)
    feats = feat_taps[0] * ext[fh:fh + rows + fh]
    for d in range(1, feat_len):
        feats = feats + feat_taps[d] * ext[fh - d:fh - d + rows + fh]
    query = feats[:rows, 0]
    key_ext = feats[:, 1]
    value_ext = feats[:, 2]
    key_feat = key_ext[:rows]
    value_feat = value_ext[:rows]
    product = key_feat * value_feat

    prev_prod = lax.ppermute(product[rows - lh:], "seq", fwd)
    pext = jnp.concatenate(
        [prev_prod, product, jnp.zeros((ext_len - rows - lh, channels), jnp.float32)], axis=0
    )
    conv = toeplitz_conv(base_fwd, pext, fwd_rows)
    mixed = (query * conv).astype(jnp.bfloat16)

    partial = jnp.einsum(
        "tc,cd->td", mixed, out_weight, preferred_element_type=jnp.float32
    ).astype(jnp.bfloat16)
    output = lax.psum_scatter(partial, "tp", scatter_dimension=1, tiled=True)

    query, key_ext, value_ext, conv = lax.optimization_barrier(
        (query, key_ext, value_ext, conv)
    )
    cot_full = lax.all_gather(cotangent, "tp", axis=1, tiled=True)
    grad_mixed = jnp.einsum(
        "te,ce->tc", cot_full, out_weight, preferred_element_type=jnp.float32
    )
    signal_grad = grad_mixed * query
    query_grad = grad_mixed * conv
    next_sig, next_qg = lax.ppermute((signal_grad[:reach], query_grad[:fh]), "seq", bwd)
    sext = jnp.concatenate(
        [signal_grad, next_sig, jnp.zeros((ext_len - rows - reach, channels), jnp.float32)], axis=0
    )
    conv_grad = toeplitz_conv(base_bwd, sext, bwd_rows)[:rows + fh]
    qg_ext = jnp.concatenate([query_grad, next_qg], axis=0)
    dext = jnp.stack([qg_ext, conv_grad * value_ext, conv_grad * key_ext], axis=1)
    igrad = feat_taps[0] * dext[:rows]
    for d in range(1, feat_len):
        igrad = igrad + feat_taps[d] * dext[d:d + rows]
    return output, igrad.astype(jnp.bfloat16)


def solution(mesh):
    in_specs = (
        P("seq", None, "tp"),
        P(None, None, "tp"),
        P("tp", None),
        P("tp", None),
        P("seq", "tp"),
    )
    out_specs = (P("seq", "tp"), P("seq", None, "tp"))
    return jax.shard_map(block, mesh=mesh, in_specs=in_specs, out_specs=out_specs, check_vma=False)
```

profile of v0, /device:TPU:0, one launch (start us, length us, event | category | flops | bytes accessed | tf_op | source)
XLA Modules:
  0.0 148.3 jit_solution(4567823042550870261)
XLA Ops:
  7.2 1.0 fusion.13
  8.2 1.3 collective-permute-start.1
  9.5 3.0 %collective-permute-start = (bf16[6,3,2048]{2,0,1:T(8,128)(2,1)S(1)}, bf16[6,3,2048]{2,0,1:T(8,128)(2,1)S(1)}, u32[]{:S(2)}, u32[]{:S(2)}) collective-permute-start(bf16[6,3,2048]{2,0,1:T(8,128)(2,1)S(1)} %get-tuple-element.14), channel_id=1, source_target_pairs={{0,4},{4,8},{8,12},{12,16},{16,20},{20,24},{24,28},{1,5},{5,9},{9,... | collective-permute-start | bytes 221192 | tf_op jit(solution)/shard_map/ppermute | solution.py:83
  12.6 1.8 %fusion.15 = (f32[1,3,2048]{2,0,1:T(1,128)S(1)}, f32[1,3,2048]{2,0,1:T(1,128)S(1)}, f32[1,3,2048]{2,0,1:T(1,128)S(1)}, f32[1,3,2048]{2,0,1:T(1,128)S(1)}, f32[1,...) fusion(f32[7,3,2048]{2,0,1:T(8,128)} %param.6), kind=kLoop, calls=%fused_computation.52 | loop fusion | bytes 344064 | tf_op jit(solution)/shard_map/slice | solution.py:86
  14.6 2.5 %maximum_convert_fusion = f32[204,3,2048]{2,0,1:T(8,128)S(1)} fusion(bf16[6,3,2048]{2,0,1:T(8,128)(2,1)S(1)} %collective-permute-done.1, bf16[192,3,2048]{2,0,1:T(8,128)(2,1)} %param.5, bf16[6,3,2048]{2,0,1:T(8,128)(2,1)S(1)} %collective-permute-done), kind=kLoop, calls=%fused_computation.31 | loop fusion | flops 7520256 | bytes 7520256 | tf_op jit(solution)/shard_map/convert_element_type | solution.py:85
  17.0 4.0 %fusion = f32[198,3,2048]{2,0,1:T(8,128)S(1)} fusion(f32[204,3,2048]{2,0,1:T(8,128)S(1)} %maximum_convert_fusion, f32[3,2048]{1,0:T(4,128)S(1)} %get-tuple-element.27, f32[3,2048]{1,0:T(4,128)S(1)} %get-tuple-element.28, f32[3,2048]{1,0:T(4,128)S(1)} %get-tuple-element.29, f32[3,2048]{1,0:T(4,128)S(1)} %get-tuple-element.30, ...), kind=kLoop, calls=%fused_computation.2 | loop fusion | flops 15814656 | bytes 39100416 | tf_op jit(solution)/shard_map/add | solution.py:88
  21.1 1.8 %slice_bitcast_fusion.2 = (f32[192,2048]{1,0:T(8,128)}, f32[192,1,2048]{2,0,1:T(8,128)S(1)}) fusion(f32[198,3,2048]{2,0,1:T(8,128)S(1)} %fusion), kind=kLoop, calls=%fused_computation.38 | loop fusion | flops 393216 | bytes 7864320 | tf_op jit(solution)/shard_map/squeeze | solution.py:89
  22.9 1.4 slice_bitcast_fusion.3
  24.3 5.5 %collective-permute-start.2 = (f32[127,2048]{1,0:T(8,128)}, f32[127,2048]{1,0:T(8,128)}, u32[]{:S(2)}, u32[]{:S(2)}) collective-permute-start(f32[127,2048]{1,0:T(8,128)} %slice_bitcast_fusion.3), channel_id=1, source_target_pairs={{0,4},{4,8},{8,12},{12,16},{16,20},{20,24},{24,28},{1,5},{5,9},{9,... | collective-permute-start | bytes 3121160 | tf_op jit(solution)/shard_map/ppermute | solution.py:96
  29.8 0.1 rev.3
  29.9 0.1 pad.21.clone
  29.9 0.7 pad_convert_fusion.1.base_ref
  30.6 3.5 %slice_bitcast_fusion = (f32[198,2048]{1,0:T(8,128)S(1)}, f32[198,2048]{1,0:T(8,128)}) fusion(f32[198,3,2048]{2,0,1:T(8,128)} %copy-done), kind=kLoop, calls=%fused_computation.32 | loop fusion | bytes 6488064 | tf_op jit(solution)/shard_map/squeeze | solution.py:91
  34.1 3.3 %maximum_maximum_fusion.ext_ref = f32[384,2048]{1,0:T(8,128)} fusion(f32[192,2048]{1,0:T(8,128)S(1)} %bitcast.36, f32[127,2048]{1,0:T(8,128)} %collective-permute-done.2, f32[384]{0:T(512)S(1)} %pad.21.clone), kind=kLoop, calls=%fused_computation.29 | loop fusion | flops 1572864 | bytes 5760512 | tf_op jit(solution)/shard_map/concatenate | solution.py:97
  37.4 13.4 %shard_map.68 = f32[192,2048]{1,0:T(8,128)} custom-call(f32[128,256]{1,0:T(8,128)} %pad_convert_fusion.1.base_ref, f32[384,2048]{1,0:T(8,128)} %maximum_maximum_fusion.ext_ref), custom_call_target="tpu_custom_call" | custom-call | flops 3221225472 | bytes 4849664 | tf_op jit(solution)/shard_map/pallas_call | solution.py:40
  50.8 16.8 %convolution_convert_fusion = bf16[192,8192]{1,0:T(8,128)(2,1)} fusion(bf16[2048,8192]{1,0:T(8,128)(2,1)} %param.8, f32[192,2048]{1,0:T(8,128)} %shard_map.68, f32[198,3,2048]{2,0,1:T(8,128)} %copy-done), kind=kOutput, calls=%fused_computation | convolution fusion | flops 6444810240 | bytes 39845888 | tf_op jit(solution)/shard_map/tc,cd->td/dot_general | solution.py:103
  67.7 11.9 %all-gather.2.cloned.1.call-done = bf16[192,8192]{1,0:T(8,128)(2,1)} async-done(((bf16[192,2048]{1,0:T(8,128)(2,1)}), bf16[192,8192]{1,0:T(8,128)(2,1)}) %all-gather.2.cloned.1.call-update) | async-done | bytes 3145744 | tf_op jit(solution)/shard_map/all_gather | solution.py:111
  79.5 16.8 %fusion.16 = f32[192,2048]{1,0:T(8,128)S(1)} fusion(bf16[192,8192]{1,0:T(8,128)(2,1)} %all-gather.2.cloned.1.call-done, bf16[2048,8192]{1,0:T(8,128)(2,1)} %param.8), kind=kOutput, calls=%fused_computation.53 | convolution fusion | flops 6442450944 | bytes 38273024 | tf_op jit(solution)/shard_map/te,ce->tc/dot_general | solution.py:112
  96.3 0.3 fusion.14
  96.6 0.1 slice.157
  96.7 1.3 collective-permute-start.4
  98.1 1.5 collective-permute-start.3
  99.5 0.6 pad_convert_fusion.base_ref
  100.2 0.1 pad.16.clone
  100.3 1.6 %collective-permute-done.3 = f32[6,2048]{1,0:T(8,128)S(1)} collective-permute-done((f32[6,2048]{1,0:T(8,128)S(1)}, f32[6,2048]{1,0:T(8,128)S(1)}, u32[]{:S(2)}, u32[]{:S(2)}) %collective-permute-start.3) | collective-permute-done | bytes 49184 | tf_op jit(solution)/shard_map/ppermute | solution.py:117
  101.8 0.1 maximum_bitcast_fusion
  102.0 1.9 %maximum_maximum_fusion.1.ext_ref = f32[384,2048]{1,0:T(8,128)} fusion(f32[133,2048]{1,0:T(8,128)S(1)} %collective-permute-done.4, f32[192,2048]{1,0:T(8,128)S(1)} %get-tuple-element.19, f32[384]{0:T(512)S(1)} %pad.16.clone), kind=kLoop, calls=%fused_computation.30 | loop fusion | flops 1572864 | bytes 5809664 | tf_op jit(solution)/shard_map/concatenate | solution.py:118
  103.9 13.3 %shard_map.69 = f32[224,2048]{1,0:T(8,128)} custom-call(f32[128,256]{1,0:T(8,128)} %pad_convert_fusion.base_ref, f32[384,2048]{1,0:T(8,128)} %maximum_maximum_fusion.1.ext_ref), custom_call_target="tpu_custom_call" | custom-call | flops 3758096384 | bytes 5111808 | tf_op jit(solution)/shard_map/pallas_call | solution.py:40
  117.2 2.3 %multiply_bitcast_fusion.1 = (f32[198,1,2048]{2,0,1:T(8,128)S(1)}, f32[198,1,2048]{2,0,1:T(8,128)S(1)}) fusion(f32[198,2048]{1,0:T(8,128)S(1)} %get-tuple-element.8, f32[224,2048]{1,0:T(8,128)} %shard_map.69, f32[198,2048]{1,0:T(8,128)} %get-tuple-element.9), kind=kLoop, calls=%fused_computation.36 | loop fusion | flops 811008 | bytes 8110080 | tf_op jit(solution)/shard_map/stack | solution.py:123
  119.5 0.4 pad_maximum_fusion
  119.9 5.0 %fusion.7 = bf16[192,3,2048]{2,0,1:T(8,128)(2,1)} fusion(f32[198,3,2048]{2,0,1:T(8,128)S(1)} %pad_maximum_fusion, f32[3,2048]{1,0:T(4,128)S(1)} %get-tuple-element.27, f32[3,2048]{1,0:T(4,128)S(1)} %get-tuple-element.28, f32[3,2048]{1,0:T(4,128)S(1)} %get-tuple-element.29, f32[3,2048]{1,0:T(4,128)S(1)} %get-tuple-element.30, ...), kind=kLoop, calls=%fused_computation.17 | loop fusion | flops 16515072 | bytes 35561472 | tf_op jit(solution)/shard_map/convert_element_type | solution.py:127
  124.9 16.6 %reduce-scatter.2.cloned.1.call-done = bf16[192,2048]{1,0:T(8,128)(2,1)} async-done(((bf16[192,8192]{1,0:T(8,128)(2,1)}), bf16[192,2048]{1,0:T(8,128)(2,1)}) %reduce-scatter.2.cloned.1.call-update) | async-done | bytes 786448 | tf_op jit(solution)/shard_map/reduce_scatter | solution.py:106
  (24 shorter events, 0.3 us)
Async XLA Ops:
  7.2 72.4 %all-gather.2.cloned.1.call-start = ((), (), s32[]{:S(2)}) async-start(), calls=%async_computation.2 | async-start | bytes 3932160 | tf_op jit(solution)/shard_map/all_gather | solution.py:111
  8.2 6.4 %collective-permute-start.1 = (bf16[6,3,2048]{2,0,1:T(8,128)(2,1)S(1)}, bf16[6,3,2048]{2,0,1:T(8,128)(2,1)S(1)}, u32[]{:S(2)}, u32[]{:S(2)}) collective-permute-start(bf16[6,3,2048]{2,0,1:T(8,128)(2,1)S(1)} %get-tuple-element.15), channel_id=1, source_target_pairs={{4,0},{8,4},{12,8},{16,12},{20,16},{24,20},{28,24},{5,1},{9,5},{13... | collective-permute-start | bytes 221192 | tf_op jit(solution)/shard_map/ppermute | solution.py:84
  9.5 5.1 %collective-permute-start = (bf16[6,3,2048]{2,0,1:T(8,128)(2,1)S(1)}, bf16[6,3,2048]{2,0,1:T(8,128)(2,1)S(1)}, u32[]{:S(2)}, u32[]{:S(2)}) collective-permute-start(bf16[6,3,2048]{2,0,1:T(8,128)(2,1)S(1)} %get-tuple-element.14), channel_id=1, source_target_pairs={{0,4},{4,8},{8,12},{12,16},{16,20},{20,24},{24,28},{1,5},{5,9},{9,... | collective-permute-start | bytes 221192 | tf_op jit(solution)/shard_map/ppermute | solution.py:83
  12.5 128.9 %reduce-scatter.2.cloned.1.call-start = ((), (), s32[]{:S(2)}) async-start(), calls=%async_computation.1 | async-start | bytes 3932160 | tf_op jit(solution)/shard_map/reduce_scatter | solution.py:106
  21.1 3.2 %copy-start = (f32[198,3,2048]{2,0,1:T(8,128)}, f32[198,3,2048]{2,0,1:T(8,128)S(1)}, u32[]{:S(2)}) copy-start(f32[198,3,2048]{2,0,1:T(8,128)S(1)} %fusion) | copy-start | bytes 14598148
  21.1 8.7 %copy-start.3 = (f32[128,128]{1,0:T(8,128)S(1)}, f32[128,128]{1,0:T(8,128)}, u32[]{:S(2)}) copy-start(f32[128,128]{1,0:T(8,128)} %param.7) | copy-start | bytes 196612
  24.3 9.8 %collective-permute-start.2 = (f32[127,2048]{1,0:T(8,128)}, f32[127,2048]{1,0:T(8,128)}, u32[]{:S(2)}, u32[]{:S(2)}) collective-permute-start(f32[127,2048]{1,0:T(8,128)} %slice_bitcast_fusion.3), channel_id=1, source_target_pairs={{0,4},{4,8},{8,12},{12,16},{16,20},{20,24},{24,28},{1,5},{5,9},{9,... | collective-permute-start | bytes 3121160 | tf_op jit(solution)/shard_map/ppermute | solution.py:96
  67.6 28.6 %copy-start.1 = (f32[192,2048]{1,0:T(8,128)S(1)}, f32[192,2048]{1,0:T(8,128)}, u32[]{:S(2)}) copy-start(f32[192,2048]{1,0:T(8,128)} %get-tuple-element.7) | copy-start | bytes 4718596
  79.5 16.8 %copy-start.2 = (f32[192,2048]{1,0:T(8,128)S(1)}, f32[192,2048]{1,0:T(8,128)}, u32[]{:S(2)}) copy-start(f32[192,2048]{1,0:T(8,128)} %shard_map.68) | copy-start | bytes 4718596
  96.7 5.2 %collective-permute-start.4 = (f32[133,2048]{1,0:T(8,128)S(1)}, f32[133,2048]{1,0:T(8,128)S(1)}, u32[]{:S(2)}, u32[]{:S(2)}) collective-permute-start(f32[133,2048]{1,0:T(8,128)S(1)} %slice.157), channel_id=1, source_target_pairs={{4,0},{8,4},{12,8},{16,12},{20,16},{24,20},{28,24},{5,1},{9,5},{13... | collective-permute-start | bytes 3268616 | tf_op jit(solution)/shard_map/ppermute | solution.py:117
  98.1 3.8 %collective-permute-start.3 = (f32[6,2048]{1,0:T(8,128)S(1)}, f32[6,2048]{1,0:T(8,128)S(1)}, u32[]{:S(2)}, u32[]{:S(2)}) collective-permute-start(f32[6,2048]{1,0:T(8,128)S(1)} %slice.156), channel_id=1, source_target_pairs={{4,0},{8,4},{12,8},{16,12},{20,16},{24,20},{28,24},{5,1},{9,5},{13... | collective-permute-start | bytes 147464 | tf_op jit(solution)/shard_map/ppermute | solution.py:117
Sparse Core Ops, SparseCore 0:
  12.7 66.8 all-gather.1
  82.4 59.0 reduce-scatter.1
where the time goes:
time: 149 us; the launch traced here: 148 us
  matrix products  33.6 us (23%)
  waiting for transfers between devices  30.1 us (20%)
  Pallas kernels  26.7 us (18%)
  other arithmetic  22.9 us (15%)
  between operations  14.3 us (10%)
  starting transfers between devices  12.6 us (8%)
  local copies, waits for them, and re-layouts  8.14 us (5%)
    pallas_call x2, Pallas kernels, toeplitz_conv(): pl.pallas_call(_toeplitz_kernel, grid=(steps,), in_specs=[pl.BlockSpec((g...  26.7 us
    dot_general x1, matrix products, block(): jnp.einsum('tc,cd->td', mixed, out_weight, preferred_element_type=jnp.flo...  16.8 us
    dot_general x1, matrix products, block(): jnp.einsum('te,ce->tc', cot_full, out_weight, preferred_element_type=jnp....  16.8 us
    reduce_scatter x1, waiting for transfers between devices, block(): output = lax.psum_scatter(partial, 'tp', scatter_dimension=1, tiled=True)  16.6 us
    all_gather x1, waiting for transfers between devices, block(): cot_full = lax.all_gather(cotangent, 'tp', axis=1, tiled=True)  11.9 us
    ppermute x1, starting transfers between devices, block(): prev_prod = lax.ppermute(product[rows - lh:], 'seq', fwd)  5.46 us
    convert_element_type x1, other arithmetic, block(): return (output, igrad.astype(jnp.bfloat16))  4.96 us
    add x1, other arithmetic, block(): feats = feats + feat_taps[d] * ext[fh - d:fh - d + rows + fh]  4.03 us
  transfers between devices with their start and end apart: 7, of which 3 were waited for; matrix products, arithmetic and copies ran while one was open for 43% of the time, Pallas kernels for 18%

commit v1 on v0

--- a/solution.py
+++ b/solution.py
@@ -21,9 +21,12 @@
     acc = jnp.zeros((half, 2 * width), jnp.float32)
     for g in range(gb):
         t = jnp.broadcast_to(base_ref[pl.ds(g, 1), :], (half, span))
-        t = pltpu.roll(t, 0, 1, stride=1, stride_axis=0).astype(jnp.bfloat16)
-        res = jnp.dot(t, p_hi, preferred_element_type=jnp.float32)
-        res = res + jnp.dot(t, p_lo, preferred_element_type=jnp.float32)
+        t = pltpu.roll(t, 0, 1, stride=1, stride_axis=0)
+        t_hi = t.astype(jnp.bfloat16)
+        t_lo = (t - t_hi.astype(jnp.float32)).astype(jnp.bfloat16)
+        res = jnp.dot(t_hi, p_hi, preferred_element_type=jnp.float32)
+        res = res + jnp.dot(t_hi, p_lo, preferred_element_type=jnp.float32)
+        res = res + jnp.dot(t_lo, p_hi, preferred_element_type=jnp.float32)
         acc = jnp.where(lane_group == g, res, acc)
     out_ref[pl.ds(0, half), :] = acc[:, :width]
     out_ref[pl.ds(half, half), :] = acc[:, width:]
@@ -36,7 +39,7 @@
     assert rows % 32 == 0 and half + span <= length and span >= half + LANES - 1
     gb = groups * LANES // channels
     steps = channels // LANES
-    flops = 4 * half * span * 2 * LANES * gb * steps
+    flops = 6 * half * span * 2 * LANES * gb * steps
     return pl.pallas_call(
         _toeplitz_kernel,
         grid=(steps,),
@@ -75,10 +78,8 @@
     bwd_rows = -(-(rows + fh) // 32) * 32
     span_f = -(-(fwd_rows // 2 + lh) // LANES) * LANES
     span_b = -(-(bwd_rows // 2 + lh) // LANES) * LANES
-    base_fwd = jnp.pad(filters[:, ::-1], ((0, 0), (0, span_f - filt_len))).astype(jnp.bfloat16)
-    base_bwd = jnp.pad(filters, ((0, 0), (0, span_b - filt_len))).astype(jnp.bfloat16)
-    base_fwd = base_fwd.astype(jnp.float32)
-    base_bwd = base_bwd.astype(jnp.float32)
+    base_fwd = jnp.pad(filters[:, ::-1], ((0, 0), (0, span_f - filt_len)))
+    base_bwd = jnp.pad(filters, ((0, 0), (0, span_b - filt_len)))
 
     prev_proj = lax.ppermute(projected[rows - fh:], "seq", fwd)
     next_proj = lax.ppermute(projected[:fh], "seq", bwd)

time: 149 us -> 150 us (level)
  Pallas kernels: 26.7 us -> 29.4 us
  waiting for transfers between devices: 30.1 us -> 27.8 us
    pallas_call x2, Pallas kernels: 26.7 us -> 29.4 us  [toeplitz_conv(): pl.pallas_call(_toeplitz_kernel, grid=(steps,), in_specs=[pl.BlockSpec((g...]
  transfers between devices with their start and end apart: 7 -> 7, of which waited for: 3 -> 3; matrix products, arithmetic and copies ran while one was open for 43% -> 43% of each run, Pallas kernels for 18% -> 20%
where the time goes in v1:
time: 150 us; the launch traced here: 149 us
  matrix products  33.8 us (23%)
  Pallas kernels  29.4 us (20%)
  waiting for transfers between devices  27.8 us (19%)
  other arithmetic  21.5 us (14%)
  between operations  14.2 us (9%)
  starting transfers between devices  12.6 us (8%)
  local copies, waits for them, and re-layouts  9.46 us (6%)
    pallas_call x2, Pallas kernels, toeplitz_conv(): pl.pallas_call(_toeplitz_kernel, grid=(steps,), in_specs=[pl.BlockSpec((g...  29.4 us
    dot_general x1, matrix products, block(): jnp.einsum('te,ce->tc', cot_full, out_weight, preferred_element_type=jnp....  17 us
    dot_general x1, matrix products, block(): jnp.einsum('tc,cd->td', mixed, out_weight, preferred_element_type=jnp.flo...  16.8 us
    reduce_scatter x1, waiting for transfers between devices, block(): output = lax.psum_scatter(partial, 'tp', scatter_dimension=1, tiled=True)  15.6 us
    all_gather x1, waiting for transfers between devices, block(): cot_full = lax.all_gather(cotangent, 'tp', axis=1, tiled=True)  10.6 us
    ppermute x1, starting transfers between devices, block(): prev_prod = lax.ppermute(product[rows - lh:], 'seq', fwd)  5.46 us
    convert_element_type x1, other arithmetic, block(): return (output, igrad.astype(jnp.bfloat16))  4.96 us
    add x1, other arithmetic, block(): feats = feats + feat_taps[d] * ext[fh - d:fh - d + rows + fh]  4.03 us
  transfers between devices with their start and end apart: 7, of which 3 were waited for; matrix products, arithmetic and copies ran while one was open for 43% of the time, Pallas kernels for 20%

profile of v1, /device:TPU:0, one launch (start us, length us, event | category | flops | bytes accessed | tf_op | source)
XLA Modules:
  0.0 148.8 jit_solution(18400005203156060753)
XLA Ops:
  7.2 1.0 fusion.13
  8.2 1.3 collective-permute-start.1
  9.5 3.0 %collective-permute-start = (bf16[6,3,2048]{2,0,1:T(8,128)(2,1)S(1)}, bf16[6,3,2048]{2,0,1:T(8,128)(2,1)S(1)}, u32[]{:S(2)}, u32[]{:S(2)}) collective-permute-start(bf16[6,3,2048]{2,0,1:T(8,128)(2,1)S(1)} %get-tuple-element.14), channel_id=1, source_target_pairs={{0,4},{4,8},{8,12},{12,16},{16,20},{20,24},{24,28},{1,5},{5,9},{9,... | collective-permute-start | bytes 221192 | tf_op jit(solution)/shard_map/ppermute | solution.py:84
  12.6 1.8 %fusion.15 = (f32[1,3,2048]{2,0,1:T(1,128)S(1)}, f32[1,3,2048]{2,0,1:T(1,128)S(1)}, f32[1,3,2048]{2,0,1:T(1,128)S(1)}, f32[1,3,2048]{2,0,1:T(1,128)S(1)}, f32[1,...) fusion(f32[7,3,2048]{2,0,1:T(8,128)} %param.6), kind=kLoop, calls=%fused_computation.50 | loop fusion | bytes 344064 | tf_op jit(solution)/shard_map/slice | solution.py:87
  14.6 2.5 %maximum_convert_fusion = f32[204,3,2048]{2,0,1:T(8,128)S(1)} fusion(bf16[6,3,2048]{2,0,1:T(8,128)(2,1)S(1)} %collective-permute-done.1, bf16[192,3,2048]{2,0,1:T(8,128)(2,1)} %param.5, bf16[6,3,2048]{2,0,1:T(8,128)(2,1)S(1)} %collective-permute-done), kind=kLoop, calls=%fused_computation.31 | loop fusion | flops 7520256 | bytes 7520256 | tf_op jit(solution)/shard_map/convert_element_type | solution.py:86
  17.0 4.0 %fusion = f32[198,3,2048]{2,0,1:T(8,128)S(1)} fusion(f32[204,3,2048]{2,0,1:T(8,128)S(1)} %maximum_convert_fusion, f32[3,2048]{1,0:T(4,128)S(1)} %get-tuple-element.27, f32[3,2048]{1,0:T(4,128)S(1)} %get-tuple-element.28, f32[3,2048]{1,0:T(4,128)S(1)} %get-tuple-element.29, f32[3,2048]{1,0:T(4,128)S(1)} %get-tuple-element.30, ...), kind=kLoop, calls=%fused_computation.2 | loop fusion | flops 15814656 | bytes 39100416 | tf_op jit(solution)/shard_map/add | solution.py:89
  21.1 1.8 %slice_bitcast_fusion.2 = (f32[192,2048]{1,0:T(8,128)}, f32[192,1,2048]{2,0,1:T(8,128)S(1)}) fusion(f32[198,3,2048]{2,0,1:T(8,128)S(1)} %fusion), kind=kLoop, calls=%fused_computation.38 | loop fusion | flops 393216 | bytes 7864320 | tf_op jit(solution)/shard_map/squeeze | solution.py:90
  22.9 1.4 slice_bitcast_fusion.3
  24.3 5.5 %collective-permute-start.2 = (f32[127,2048]{1,0:T(8,128)}, f32[127,2048]{1,0:T(8,128)}, u32[]{:S(2)}, u32[]{:S(2)}) collective-permute-start(f32[127,2048]{1,0:T(8,128)} %slice_bitcast_fusion.3), channel_id=1, source_target_pairs={{0,4},{4,8},{8,12},{12,16},{16,20},{20,24},{24,28},{1,5},{5,9},{9,... | collective-permute-start | bytes 3121160 | tf_op jit(solution)/shard_map/ppermute | solution.py:97
  29.8 0.1 rev.3
  29.8 0.7 pad.7.base_ref
  30.5 0.1 pad.19.clone
  30.6 3.5 %slice_bitcast_fusion = (f32[198,2048]{1,0:T(8,128)S(1)}, f32[198,2048]{1,0:T(8,128)}) fusion(f32[198,3,2048]{2,0,1:T(8,128)} %copy-done), kind=kLoop, calls=%fused_computation.32 | loop fusion | bytes 6488064 | tf_op jit(solution)/shard_map/squeeze | solution.py:92
  34.1 3.3 %maximum_maximum_fusion.ext_ref = f32[384,2048]{1,0:T(8,128)} fusion(f32[192,2048]{1,0:T(8,128)S(1)} %bitcast.36, f32[127,2048]{1,0:T(8,128)} %collective-permute-done.2, f32[384]{0:T(512)S(1)} %pad.19.clone), kind=kLoop, calls=%fused_computation.29 | loop fusion | flops 1572864 | bytes 5760512 | tf_op jit(solution)/shard_map/concatenate | solution.py:98
  37.4 14.8 %shard_map.68 = f32[192,2048]{1,0:T(8,128)} custom-call(f32[128,256]{1,0:T(8,128)} %pad.7.base_ref, f32[384,2048]{1,0:T(8,128)} %maximum_maximum_fusion.ext_ref), custom_call_target="tpu_custom_call" | custom-call | flops 4831838208 | bytes 4849664 | tf_op jit(solution)/shard_map/pallas_call | solution.py:43
  52.1 16.8 %convolution_convert_fusion = bf16[192,8192]{1,0:T(8,128)(2,1)} fusion(bf16[2048,8192]{1,0:T(8,128)(2,1)} %param.8, f32[192,2048]{1,0:T(8,128)} %shard_map.68, f32[198,3,2048]{2,0,1:T(8,128)} %copy-done), kind=kOutput, calls=%fused_computation | convolution fusion | flops 6444810240 | bytes 39845888 | tf_op jit(solution)/shard_map/tc,cd->td/dot_general | solution.py:104
  69.0 10.6 %all-gather.2.cloned.1.call-done = bf16[192,8192]{1,0:T(8,128)(2,1)} async-done(((bf16[192,2048]{1,0:T(8,128)(2,1)}), bf16[192,8192]{1,0:T(8,128)(2,1)}) %all-gather.2.cloned.1.call-update) | async-done | bytes 3145744 | tf_op jit(solution)/shard_map/all_gather | solution.py:112
  79.5 17.0 %fusion.16 = f32[192,2048]{1,0:T(8,128)S(1)} fusion(bf16[192,8192]{1,0:T(8,128)(2,1)} %all-gather.2.cloned.1.call-done, bf16[2048,8192]{1,0:T(8,128)(2,1)} %param.8), kind=kOutput, calls=%fused_computation.51 | convolution fusion | flops 6442450944 | bytes 38273024 | tf_op jit(solution)/shard_map/te,ce->tc/dot_general | solution.py:113
  96.5 0.3 fusion.14
  96.9 0.1 slice.157
  97.0 1.3 collective-permute-start.4
  98.3 1.5 collective-permute-start.3
  99.7 0.7 pad.8.base_ref
  100.4 0.1 pad.14.clone
  100.5 1.6 %collective-permute-done.3 = f32[6,2048]{1,0:T(8,128)S(1)} collective-permute-done((f32[6,2048]{1,0:T(8,128)S(1)}, f32[6,2048]{1,0:T(8,128)S(1)}, u32[]{:S(2)}, u32[]{:S(2)}) %collective-permute-start.3) | collective-permute-done | bytes 49184 | tf_op jit(solution)/shard_map/ppermute | solution.py:118
  102.0 0.1 maximum_bitcast_fusion
  102.2 1.9 %maximum_maximum_fusion.1.ext_ref = f32[384,2048]{1,0:T(8,128)} fusion(f32[133,2048]{1,0:T(8,128)S(1)} %collective-permute-done.4, f32[192,2048]{1,0:T(8,128)S(1)} %get-tuple-element.19, f32[384]{0:T(512)S(1)} %pad.14.clone), kind=kLoop, calls=%fused_computation.30 | loop fusion | flops 1572864 | bytes 5809664 | tf_op jit(solution)/shard_map/concatenate | solution.py:119
  104.1 14.6 %shard_map.69 = f32[224,2048]{1,0:T(8,128)} custom-call(f32[128,256]{1,0:T(8,128)} %pad.8.base_ref, f32[384,2048]{1,0:T(8,128)} %maximum_maximum_fusion.1.ext_ref), custom_call_target="tpu_custom_call" | custom-call | flops 5637144576 | bytes 5111808 | tf_op jit(solution)/shard_map/pallas_call | solution.py:43
  118.7 2.3 %multiply_bitcast_fusion.1 = (f32[198,1,2048]{2,0,1:T(8,128)S(1)}, f32[198,1,2048]{2,0,1:T(8,128)S(1)}) fusion(f32[198,2048]{1,0:T(8,128)S(1)} %get-tuple-element.8, f32[224,2048]{1,0:T(8,128)} %shard_map.69, f32[198,2048]{1,0:T(8,128)} %get-tuple-element.9), kind=kLoop, calls=%fused_computation.36 | loop fusion | flops 811008 | bytes 8110080 | tf_op jit(solution)/shard_map/stack | solution.py:124
  121.0 0.4 pad_maximum_fusion
  121.4 5.0 %fusion.7 = bf16[192,3,2048]{2,0,1:T(8,128)(2,1)} fusion(f32[198,3,2048]{2,0,1:T(8,128)S(1)} %pad_maximum_fusion, f32[3,2048]{1,0:T(4,128)S(1)} %get-tuple-element.27, f32[3,2048]{1,0:T(4,128)S(1)} %get-tuple-element.28, f32[3,2048]{1,0:T(4,128)S(1)} %get-tuple-element.29, f32[3,2048]{1,0:T(4,128)S(1)} %get-tuple-element.30, ...), kind=kLoop, calls=%fused_computation.17 | loop fusion | flops 16515072 | bytes 35561472 | tf_op jit(solution)/shard_map/convert_element_type | solution.py:128
  126.3 15.6 %reduce-scatter.2.cloned.1.call-done = bf16[192,2048]{1,0:T(8,128)(2,1)} async-done(((bf16[192,8192]{1,0:T(8,128)(2,1)}), bf16[192,2048]{1,0:T(8,128)(2,1)}) %reduce-scatter.2.cloned.1.call-update) | async-done | bytes 786448 | tf_op jit(solution)/shard_map/reduce_scatter | solution.py:107
  (23 shorter events, 0.3 us)
Async XLA Ops:
  7.2 72.4 %all-gather.2.cloned.1.call-start = ((), (), s32[]{:S(2)}) async-start(), calls=%async_computation.2 | async-start | bytes 3932160 | tf_op jit(solution)/shard_map/all_gather | solution.py:112
  8.2 6.4 %collective-permute-start.1 = (bf16[6,3,2048]{2,0,1:T(8,128)(2,1)S(1)}, bf16[6,3,2048]{2,0,1:T(8,128)(2,1)S(1)}, u32[]{:S(2)}, u32[]{:S(2)}) collective-permute-start(bf16[6,3,2048]{2,0,1:T(8,128)(2,1)S(1)} %get-tuple-element.15), channel_id=1, source_target_pairs={{4,0},{8,4},{12,8},{16,12},{20,16},{24,20},{28,24},{5,1},{9,5},{13... | collective-permute-start | bytes 221192 | tf_op jit(solution)/shard_map/ppermute | solution.py:85
  9.5 5.1 %collective-permute-start = (bf16[6,3,2048]{2,0,1:T(8,128)(2,1)S(1)}, bf16[6,3,2048]{2,0,1:T(8,128)(2,1)S(1)}, u32[]{:S(2)}, u32[]{:S(2)}) collective-permute-start(bf16[6,3,2048]{2,0,1:T(8,128)(2,1)S(1)} %get-tuple-element.14), channel_id=1, source_target_pairs={{0,4},{4,8},{8,12},{12,16},{16,20},{20,24},{24,28},{1,5},{5,9},{9,... | collective-permute-start | bytes 221192 | tf_op jit(solution)/shard_map/ppermute | solution.py:84
  12.5 129.4 %reduce-scatter.2.cloned.1.call-start = ((), (), s32[]{:S(2)}) async-start(), calls=%async_computation.1 | async-start | bytes 3932160 | tf_op jit(solution)/shard_map/reduce_scatter | solution.py:107
  21.1 3.2 %copy-start = (f32[198,3,2048]{2,0,1:T(8,128)}, f32[198,3,2048]{2,0,1:T(8,128)S(1)}, u32[]{:S(2)}) copy-start(f32[198,3,2048]{2,0,1:T(8,128)S(1)} %fusion) | copy-start | bytes 14598148
  21.1 8.7 %copy-start.3 = (f32[128,128]{1,0:T(8,128)S(1)}, f32[128,128]{1,0:T(8,128)}, u32[]{:S(2)}) copy-start(f32[128,128]{1,0:T(8,128)} %param.7) | copy-start | bytes 196612
  24.3 9.8 %collective-permute-start.2 = (f32[127,2048]{1,0:T(8,128)}, f32[127,2048]{1,0:T(8,128)}, u32[]{:S(2)}, u32[]{:S(2)}) collective-permute-start(f32[127,2048]{1,0:T(8,128)} %slice_bitcast_fusion.3), channel_id=1, source_target_pairs={{0,4},{4,8},{8,12},{12,16},{16,20},{20,24},{24,28},{1,5},{5,9},{9,... | collective-permute-start | bytes 3121160 | tf_op jit(solution)/shard_map/ppermute | solution.py:97
  69.0 27.6 %copy-start.1 = (f32[192,2048]{1,0:T(8,128)S(1)}, f32[192,2048]{1,0:T(8,128)}, u32[]{:S(2)}) copy-start(f32[192,2048]{1,0:T(8,128)} %get-tuple-element.7) | copy-start | bytes 4718596
  79.5 17.0 %copy-start.2 = (f32[192,2048]{1,0:T(8,128)S(1)}, f32[192,2048]{1,0:T(8,128)}, u32[]{:S(2)}) copy-start(f32[192,2048]{1,0:T(8,128)} %shard_map.68) | copy-start | bytes 4718596
  97.0 5.2 %collective-permute-start.4 = (f32[133,2048]{1,0:T(8,128)S(1)}, f32[133,2048]{1,0:T(8,128)S(1)}, u32[]{:S(2)}, u32[]{:S(2)}) collective-permute-start(f32[133,2048]{1,0:T(8,128)S(1)} %slice.157), channel_id=1, source_target_pairs={{4,0},{8,4},{12,8},{16,12},{20,16},{24,20},{28,24},{5,1},{9,5},{13... | collective-permute-start | bytes 3268616 | tf_op jit(solution)/shard_map/ppermute | solution.py:118
  98.3 3.8 %collective-permute-start.3 = (f32[6,2048]{1,0:T(8,128)S(1)}, f32[6,2048]{1,0:T(8,128)S(1)}, u32[]{:S(2)}, u32[]{:S(2)}) collective-permute-start(f32[6,2048]{1,0:T(8,128)S(1)} %slice.156), channel_id=1, source_target_pairs={{4,0},{8,4},{12,8},{16,12},{20,16},{24,20},{28,24},{5,1},{9,5},{13... | collective-permute-start | bytes 147464 | tf_op jit(solution)/shard_map/ppermute | solution.py:118
Sparse Core Ops, SparseCore 0:
  12.7 66.8 all-gather.1
  82.4 59.5 reduce-scatter.1

commit v2 on v0

--- a/solution.py
+++ b/solution.py
@@ -58,6 +58,26 @@
     return [(j + 1, j) for j in range(n - 1)]
 
 
+def tp_reduce_scatter(part, axis_name):
+    n = lax.axis_size(axis_name)
+    if n > 8:
+        return lax.psum_scatter(part, axis_name, scatter_dimension=1, tiled=True)
+    k = lax.axis_index(axis_name)
+    width = part.shape[1] // n
+    recv_r = jnp.zeros((part.shape[0], width), part.dtype)
+    recv_l = recv_r
+    for s in range(1, n):
+        blk_r = lax.dynamic_slice_in_dim(part, (k + n - s) * width, width, axis=1)
+        blk_l = lax.dynamic_slice_in_dim(part, jnp.maximum(k - (n - s), 0) * width, width, axis=1)
+        msg_r = (blk_r.astype(jnp.float32) + recv_r.astype(jnp.float32)).astype(part.dtype)
+        msg_l = (blk_l.astype(jnp.float32) + recv_l.astype(jnp.float32)).astype(part.dtype)
+        recv_r = lax.ppermute(msg_r, axis_name, [(j, j + 1) for j in range(0, s)])
+        recv_l = lax.ppermute(msg_l, axis_name, [(j, j - 1) for j in range(n - s, n)])
+    own = lax.dynamic_slice_in_dim(part, k * width, width, axis=1)
+    total = own.astype(jnp.float32) + recv_r.astype(jnp.float32) + recv_l.astype(jnp.float32)
+    return total.astype(part.dtype)
+
+
 def block(projected, feat_taps, filters, out_weight, cotangent):
     rows = projected.shape[0]
     feat_len = feat_taps.shape[0]
@@ -103,15 +123,13 @@
     partial = jnp.einsum(
         "tc,cd->td", mixed, out_weight, preferred_element_type=jnp.float32
     ).astype(jnp.bfloat16)
-    output = lax.psum_scatter(partial, "tp", scatter_dimension=1, tiled=True)
+    output = tp_reduce_scatter(partial, "tp")
 
     query, key_ext, value_ext, conv = lax.optimization_barrier(
         (query, key_ext, value_ext, conv)
     )
     cot_full = lax.all_gather(cotangent, "tp", axis=1, tiled=True)
-    grad_mixed = jnp.einsum(
-        "te,ce->tc", cot_full, out_weight, preferred_element_type=jnp.float32
-    )
+    grad_mixed = jnp.einsum("te,ce->tc", cot_full, out_weight, preferred_element_type=jnp.float32)
     signal_grad = grad_mixed * query
     query_grad = grad_mixed * conv
     next_sig, next_qg = lax.ppermute((signal_grad[:reach], query_grad[:fh]), "seq", bwd)

time: 149 us -> 232 us (1.56)
  the two profiles are of different devices: /device:TPU:0 before, /device:TPU:17 now
where the time goes in v2:
time: 232 us; the launch traced here: 231 us
  waiting for transfers between devices  82.1 us (35%)
  other arithmetic  37.3 us (16%)
  matrix products  31.6 us (14%)
  starting transfers between devices  27.7 us (12%)
  Pallas kernels  26.9 us (12%)
  between operations  14.3 us (6%)
  local copies, waits for them, and re-layouts  10.7 us (5%)
    ppermute x3, waiting for transfers between devices, tp_reduce_scatter(): lax.ppermute(msg_l, axis_name, [(j, j - 1) for j in range(n - s, n)])  33.2 us
    pallas_call x2, Pallas kernels, toeplitz_conv(): pl.pallas_call(_toeplitz_kernel, grid=(steps,), in_specs=[pl.BlockSpec((g...  26.9 us
    ppermute x2, waiting for transfers between devices, block(): lax.ppermute((signal_grad[:reach], query_grad[:fh]), 'seq', bwd)  24 us
    dot_general x1, matrix products, block(): jnp.einsum('te,ce->tc', cot_full, out_weight, preferred_element_type=jnp....  16.5 us
    dot_general x1, matrix products, block(): jnp.einsum('tc,cd->td', mixed, out_weight, preferred_element_type=jnp.flo...  15 us
    ppermute x3, waiting for transfers between devices, tp_reduce_scatter(): recv_r = lax.ppermute(msg_r, axis_name, [(j, j + 1) for j in range(0, s)])  14 us
    ppermute x1, waiting for transfers between devices, block(): prev_prod = lax.ppermute(product[rows - lh:], 'seq', fwd)  10.8 us
    ppermute x3, starting transfers between devices, tp_reduce_scatter(): lax.ppermute(msg_l, axis_name, [(j, j - 1) for j in range(n - s, n)])  8.63 us
  transfers between devices with their start and end apart: 12, of which 5 were waited for; matrix products, arithmetic and copies ran while one was open for 26% of the time, Pallas kernels for 6%

profile of v2, /device:TPU:17, one launch (start us, length us, event | category | flops | bytes accessed | tf_op | source)
XLA Modules:
  0.0 230.6 jit_solution(5283132181222878302)
XLA Ops:
  8.2 2.6 %collective-permute-start.1 = (bf16[6,3,2048]{2,0,1:T(8,128)(2,1)S(1)}, bf16[6,3,2048]{2,0,1:T(8,128)(2,1)S(1)}, u32[]{:S(2)}, u32[]{:S(2)}) collective-permute-start(bf16[6,3,2048]{2,0,1:T(8,128)(2,1)S(1)} %get-tuple-element.19), channel_id=1, source_target_pairs={{4,0},{8,4},{12,8},{16,12},{20,16},{24,20},{28,24},{5,1},{9,5},{13... | collective-permute-start | bytes 221192 | tf_op jit(solution)/shard_map/ppermute | solution.py:104
  10.8 3.0 %collective-permute-start = (bf16[6,3,2048]{2,0,1:T(8,128)(2,1)S(1)}, bf16[6,3,2048]{2,0,1:T(8,128)(2,1)S(1)}, u32[]{:S(2)}, u32[]{:S(2)}) collective-permute-start(bf16[6,3,2048]{2,0,1:T(8,128)(2,1)S(1)} %get-tuple-element.18), channel_id=1, source_target_pairs={{0,4},{4,8},{8,12},{12,16},{16,20},{20,24},{24,28},{1,5},{5,9},{9,... | collective-permute-start | bytes 221192 | tf_op jit(solution)/shard_map/ppermute | solution.py:103
  13.8 1.8 fusion.15
  15.8 2.5 %maximum_convert_fusion = f32[204,3,2048]{2,0,1:T(8,128)S(1)} fusion(bf16[6,3,2048]{2,0,1:T(8,128)(2,1)S(1)} %collective-permute-done.1, bf16[192,3,2048]{2,0,1:T(8,128)(2,1)} %param.5, bf16[6,3,2048]{2,0,1:T(8,128)(2,1)S(1)} %collective-permute-done), kind=kLoop, calls=%fused_computation.31 | loop fusion | flops 7520256 | bytes 7520256 | tf_op jit(solution)/shard_map/convert_element_type | solution.py:105
  18.2 4.0 %fusion = f32[198,3,2048]{2,0,1:T(8,128)S(1)} fusion(f32[204,3,2048]{2,0,1:T(8,128)S(1)} %maximum_convert_fusion, f32[3,2048]{1,0:T(4,128)S(1)} %get-tuple-element.31, f32[3,2048]{1,0:T(4,128)S(1)} %get-tuple-element.32, f32[3,2048]{1,0:T(4,128)S(1)} %get-tuple-element.33, f32[3,2048]{1,0:T(4,128)S(1)} %get-tuple-element.34, ...), kind=kLoop, calls=%fused_computation.2 | loop fusion | flops 15814656 | bytes 39100416 | tf_op jit(solution)/shard_map/add | solution.py:108
  22.3 1.8 slice_bitcast_fusion.2
  25.1 3.9 %collective-permute-start.2 = (f32[127,2048]{1,0:T(8,128)S(1)}, f32[127,2048]{1,0:T(8,128)}, u32[]{:S(2)}, u32[]{:S(2)}) collective-permute-start(f32[127,2048]{1,0:T(8,128)S(1)} %slice_bitcast_fusion.3), channel_id=1, source_target_pairs={{0,4},{4,8},{8,12},{12,16},{16,20},{20,24},{24,28},{1,5},{5,9},{9,... | collective-permute-start | bytes 3121160 | tf_op jit(solution)/shard_map/ppermute | solution.py:116
  29.9 10.8 %collective-permute-done.2 = f32[127,2048]{1,0:T(8,128)} collective-permute-done((f32[127,2048]{1,0:T(8,128)S(1)}, f32[127,2048]{1,0:T(8,128)}, u32[]{:S(2)}, u32[]{:S(2)}) %collective-permute-start.2) | collective-permute-done | bytes 1040416 | tf_op jit(solution)/shard_map/ppermute | solution.py:116
  40.8 3.3 %maximum_maximum_fusion.ext_ref = f32[384,2048]{1,0:T(8,128)} fusion(f32[192,2048]{1,0:T(8,128)S(1)} %bitcast.36, f32[127,2048]{1,0:T(8,128)} %collective-permute-done.2, f32[384]{0:T(512)S(1)} %pad.21.clone), kind=kLoop, calls=%fused_computation.29 | loop fusion | flops 1572864 | bytes 5760512 | tf_op jit(solution)/shard_map/concatenate | solution.py:117
  44.0 13.4 %shard_map.68 = f32[192,2048]{1,0:T(8,128)} custom-call(f32[128,256]{1,0:T(8,128)} %pad_convert_fusion.1.base_ref, f32[384,2048]{1,0:T(8,128)} %maximum_maximum_fusion.ext_ref), custom_call_target="tpu_custom_call" | custom-call | flops 3221225472 | bytes 4849664 | tf_op jit(solution)/shard_map/pallas_call | solution.py:40
  57.4 15.0 %convolution_convert_fusion = bf16[192,8192]{1,0:T(8,128)(2,1)S(1)} fusion(bf16[2048,8192]{1,0:T(8,128)(2,1)} %param.8, f32[192,2048]{1,0:T(8,128)} %shard_map.68, f32[198,3,2048]{2,0,1:T(8,128)} %copy-done), kind=kOutput, calls=%fused_computation | convolution fusion | flops 6444810240 | bytes 39845888 | tf_op jit(solution)/shard_map/tc,cd->td/dot_general | solution.py:123
  73.9 1.6 collective-permute-start.3
  76.7 2.3 add_convert_fusion.4
  80.3 29.1 %collective-permute-done.6 = bf16[192,2048]{1,0:T(8,128)(2,1)} collective-permute-done((bf16[192,2048]{1,0:T(8,128)(2,1)}, bf16[192,2048]{1,0:T(8,128)(2,1)}, u32[]{:S(2)}, u32[]{:S(2)}) %collective-permute-start.6) | collective-permute-done | bytes 786464 | tf_op jit(solution)/shard_map/ppermute | solution.py:75
  109.4 14.0 %collective-permute-done.4 = bf16[192,2048]{1,0:T(8,128)(2,1)} collective-permute-done((bf16[192,2048]{1,0:T(8,128)(2,1)}, bf16[192,2048]{1,0:T(8,128)(2,1)}, u32[]{:S(2)}, u32[]{:S(2)}) %collective-permute-start.4) | collective-permute-done | bytes 786464 | tf_op jit(solution)/shard_map/ppermute | solution.py:74
  123.4 3.1 %add_convert_fusion.3 = (bf16[192,2048]{1,0:T(8,128)(2,1)}, bf16[192,2048]{1,0:T(8,128)(2,1)}) fusion(bf16[192,2048]{1,0:T(8,128)(2,1)} %collective-permute-done.4, bf16[192,8192]{1,0:T(8,128)(2,1)S(1)} %convolution_convert_fusion, s32[]{:T(128)S(6)} %select_n.22, bf16[192,2048]{1,0:T(8,128)(2,1)} %collective-permute-done.6, s32[]{:T(128)S(6)} %select_n.26), kind=kLoop, calls=%fused_computation.42 | loop fusion | flops 3145728 | bytes 4718600 | tf_op jit(solution)/shard_map/convert_element_type | solution.py:72
  126.5 3.6 %collective-permute-start.7 = (bf16[192,2048]{1,0:T(8,128)(2,1)}, bf16[192,2048]{1,0:T(8,128)(2,1)}, u32[]{:S(2)}, u32[]{:S(2)}) collective-permute-start(bf16[192,2048]{1,0:T(8,128)(2,1)} %get-tuple-element.15), channel_id=1, source_target_pairs={{2,1},{3,2},{6,5},{7,6},{10,9},{11,10},{14,13},{15,14},{18,17},{19... | collective-permute-start | bytes 2359304 | tf_op jit(solution)/shard_map/ppermute | solution.py:75
  130.0 4.1 %slice_bitcast_fusion = (f32[198,2048]{1,0:T(8,128)}, f32[198,2048]{1,0:T(8,128)}) fusion(f32[198,3,2048]{2,0,1:T(8,128)} %copy-done), kind=kLoop, calls=%fused_computation.32 | loop fusion | bytes 6488064 | tf_op jit(solution)/shard_map/squeeze | solution.py:111
  134.1 2.6 %collective-permute-start.5 = (bf16[192,2048]{1,0:T(8,128)(2,1)}, bf16[192,2048]{1,0:T(8,128)(2,1)}, u32[]{:S(2)}, u32[]{:S(2)}) collective-permute-start(bf16[192,2048]{1,0:T(8,128)(2,1)} %get-tuple-element.14), channel_id=1, source_target_pairs={{0,1},{1,2},{2,3},{4,5},{5,6},{6,7},{8,9},{9,10},{10,11},{12,13},{... | collective-permute-start | bytes 2359304 | tf_op jit(solution)/shard_map/ppermute | solution.py:74
  136.7 4.2 %collective-permute-done.7 = bf16[192,2048]{1,0:T(8,128)(2,1)} collective-permute-done((bf16[192,2048]{1,0:T(8,128)(2,1)}, bf16[192,2048]{1,0:T(8,128)(2,1)}, u32[]{:S(2)}, u32[]{:S(2)}) %collective-permute-start.7) | collective-permute-done | bytes 786464 | tf_op jit(solution)/shard_map/ppermute | solution.py:75
  140.9 2.3 add_convert_fusion.1
  143.2 3.8 %collective-permute-start.8 = (bf16[192,2048]{1,0:T(8,128)(2,1)}, bf16[192,2048]{1,0:T(8,128)(2,1)}, u32[]{:S(2)}, u32[]{:S(2)}) collective-permute-start(bf16[192,2048]{1,0:T(8,128)(2,1)} %add_convert_fusion.1), channel_id=1, source_target_pairs={{1,0},{2,1},{3,2},{5,4},{6,5},{7,6},{9,8},{10,9},{11,10},{13,12},{... | collective-permute-start | bytes 2359304 | tf_op jit(solution)/shard_map/ppermute | solution.py:75
  147.0 16.5 %fusion.16 = f32[192,2048]{1,0:T(8,128)S(1)} fusion(bf16[192,8192]{1,0:T(8,128)(2,1)} %all-gather.2.cloned.1.call-done, bf16[2048,8192]{1,0:T(8,128)(2,1)} %param.8), kind=kOutput, calls=%fused_computation.60 | convolution fusion | flops 6442450944 | bytes 38273024 | tf_op jit(solution)/shard_map/te,ce->tc/dot_general | solution.py:132
  163.6 2.2 fusion.14
  166.9 1.9 collective-permute-start.10
  169.6 2.1 collective-permute-start.9
  171.7 2.9 %add_convert_fusion = bf16[192,2048]{1,0:T(8,128)(2,1)} fusion(bf16[192,2048]{1,0:T(8,128)(2,1)} %collective-permute-done.8, bf16[192,2048]{1,0:T(8,128)(2,1)} %collective-permute-done.5, bf16[192,8192]{1,0:T(8,128)(2,1)} %copy-done.1, s32[]{:T(128)S(6)} %select_n.21), kind=kLoop, calls=%fused_computation.39 | loop fusion | flops 2359296 | bytes 3145732 | tf_op jit(solution)/shard_map/convert_element_type | solution.py:78
  174.6 24.0 %collective-permute-done.9 = f32[6,2048]{1,0:T(8,128)S(1)} collective-permute-done((f32[6,2048]{1,0:T(8,128)S(1)}, f32[6,2048]{1,0:T(8,128)S(1)}, u32[]{:S(2)}, u32[]{:S(2)}) %collective-permute-start.9) | collective-permute-done | bytes 49184 | tf_op jit(solution)/shard_map/ppermute | solution.py:135
  199.9 3.1 %maximum_maximum_fusion.1.ext_ref = f32[384,2048]{1,0:T(8,128)} fusion(f32[133,2048]{1,0:T(8,128)} %collective-permute-done.10, f32[192,2048]{1,0:T(8,128)S(1)} %get-tuple-element.23, f32[384]{0:T(512)S(1)} %pad.16.clone), kind=kLoop, calls=%fused_computation.30 | loop fusion | flops 1572864 | bytes 5809664 | tf_op jit(solution)/shard_map/concatenate | solution.py:136
  203.0 13.4 %shard_map.69 = f32[224,2048]{1,0:T(8,128)} custom-call(f32[128,256]{1,0:T(8,128)} %pad_convert_fusion.base_ref, f32[384,2048]{1,0:T(8,128)} %maximum_maximum_fusion.1.ext_ref), custom_call_target="tpu_custom_call" | custom-call | flops 3758096384 | bytes 5111808 | tf_op jit(solution)/shard_map/pallas_call | solution.py:40
  216.5 1.9 multiply_bitcast_fusion.1
  218.8 5.0 %fusion.7 = bf16[192,3,2048]{2,0,1:T(8,128)(2,1)} fusion(f32[198,3,2048]{2,0,1:T(8,128)S(1)} %pad_maximum_fusion, f32[3,2048]{1,0:T(4,128)S(1)} %get-tuple-element.31, f32[3,2048]{1,0:T(4,128)S(1)} %get-tuple-element.32, f32[3,2048]{1,0:T(4,128)S(1)} %get-tuple-element.33, f32[3,2048]{1,0:T(4,128)S(1)} %get-tuple-element.34, ...), kind=kLoop, calls=%fused_computation.17 | loop fusion | flops 16515072 | bytes 35561472 | tf_op jit(solution)/shard_map/convert_element_type | solution.py:145
  (42 shorter events, 10.5 us)
Async XLA Ops:
  7.2 139.9 %all-gather.2.cloned.1.call-start = ((), (), s32[]{:S(2)}) async-start(), calls=%async_computation | async-start | bytes 3932160 | tf_op jit(solution)/shard_map/all_gather | solution.py:131
  8.2 7.6 %collective-permute-start.1 = (bf16[6,3,2048]{2,0,1:T(8,128)(2,1)S(1)}, bf16[6,3,2048]{2,0,1:T(8,128)(2,1)S(1)}, u32[]{:S(2)}, u32[]{:S(2)}) collective-permute-start(bf16[6,3,2048]{2,0,1:T(8,128)(2,1)S(1)} %get-tuple-element.19), channel_id=1, source_target_pairs={{4,0},{8,4},{12,8},{16,12},{20,16},{24,20},{28,24},{5,1},{9,5},{13... | collective-permute-start | bytes 221192 | tf_op jit(solution)/shard_map/ppermute | solution.py:104
  10.8 5.0 %collective-permute-start = (bf16[6,3,2048]{2,0,1:T(8,128)(2,1)S(1)}, bf16[6,3,2048]{2,0,1:T(8,128)(2,1)S(1)}, u32[]{:S(2)}, u32[]{:S(2)}) collective-permute-start(bf16[6,3,2048]{2,0,1:T(8,128)(2,1)S(1)} %get-tuple-element.18), channel_id=1, source_target_pairs={{0,4},{4,8},{8,12},{12,16},{16,20},{20,24},{24,28},{1,5},{5,9},{9,... | collective-permute-start | bytes 221192 | tf_op jit(solution)/shard_map/ppermute | solution.py:103
  22.3 2.7 %copy-start = (f32[198,3,2048]{2,0,1:T(8,128)}, f32[198,3,2048]{2,0,1:T(8,128)S(1)}, u32[]{:S(2)}) copy-start(f32[198,3,2048]{2,0,1:T(8,128)S(1)} %fusion) | copy-start | bytes 14598148
  22.3 6.8 %copy-start.5 = (f32[128,128]{1,0:T(8,128)S(1)}, f32[128,128]{1,0:T(8,128)}, u32[]{:S(2)}) copy-start(f32[128,128]{1,0:T(8,128)} %param.7) | copy-start | bytes 196612
  25.1 15.7 %collective-permute-start.2 = (f32[127,2048]{1,0:T(8,128)S(1)}, f32[127,2048]{1,0:T(8,128)}, u32[]{:S(2)}, u32[]{:S(2)}) collective-permute-start(f32[127,2048]{1,0:T(8,128)S(1)} %slice_bitcast_fusion.3), channel_id=1, source_target_pairs={{0,4},{4,8},{8,12},{12,16},{16,20},{20,24},{24,28},{1,5},{5,9},{9,... | collective-permute-start | bytes 3121160 | tf_op jit(solution)/shard_map/ppermute | solution.py:116
  72.5 68.4 %copy-start.1 = (bf16[192,8192]{1,0:T(8,128)(2,1)}, bf16[192,8192]{1,0:T(8,128)(2,1)S(1)}, u32[]{:S(2)}) copy-start(bf16[192,8192]{1,0:T(8,128)(2,1)S(1)} %convolution_convert_fusion) | copy-start | bytes 9437188
  73.9 2.9 %collective-permute-start.3 = (bf16[192,2048]{1,0:T(8,128)(2,1)}, bf16[192,2048]{1,0:T(8,128)(2,1)}, u32[]{:S(2)}, u32[]{:S(2)}) collective-permute-start(bf16[192,2048]{1,0:T(8,128)(2,1)} %get-tuple-element.16), channel_id=1, source_target_pairs={{0,1},{4,5},{8,9},{12,13},{16,17},{20,21},{24,25},{28,29}} | collective-permute-start | bytes 2359304 | tf_op jit(solution)/shard_map/ppermute | solution.py:74
  75.4 34.0 %collective-permute-start.6 = (bf16[192,2048]{1,0:T(8,128)(2,1)}, bf16[192,2048]{1,0:T(8,128)(2,1)}, u32[]{:S(2)}, u32[]{:S(2)}) collective-permute-start(bf16[192,2048]{1,0:T(8,128)(2,1)} %get-tuple-element.17), channel_id=1, source_target_pairs={{3,2},{7,6},{11,10},{15,14},{19,18},{23,22},{27,26},{31,30}} | collective-permute-start | bytes 2359304 | tf_op jit(solution)/shard_map/ppermute | solution.py:75
  79.0 44.3 %collective-permute-start.4 = (bf16[192,2048]{1,0:T(8,128)(2,1)}, bf16[192,2048]{1,0:T(8,128)(2,1)}, u32[]{:S(2)}, u32[]{:S(2)}) collective-permute-start(bf16[192,2048]{1,0:T(8,128)(2,1)} %add_convert_fusion.4), channel_id=1, source_target_pairs={{0,1},{1,2},{4,5},{5,6},{8,9},{9,10},{12,13},{13,14},{16,17},{17,1... | collective-permute-start | bytes 2359304 | tf_op jit(solution)/shard_map/ppermute | solution.py:74
  126.5 14.4 %collective-permute-start.7 = (bf16[192,2048]{1,0:T(8,128)(2,1)}, bf16[192,2048]{1,0:T(8,128)(2,1)}, u32[]{:S(2)}, u32[]{:S(2)}) collective-permute-start(bf16[192,2048]{1,0:T(8,128)(2,1)} %get-tuple-element.15), channel_id=1, source_target_pairs={{2,1},{3,2},{6,5},{7,6},{10,9},{11,10},{14,13},{15,14},{18,17},{19... | collective-permute-start | bytes 2359304 | tf_op jit(solution)/shard_map/ppermute | solution.py:75
  134.1 37.5 %collective-permute-start.5 = (bf16[192,2048]{1,0:T(8,128)(2,1)}, bf16[192,2048]{1,0:T(8,128)(2,1)}, u32[]{:S(2)}, u32[]{:S(2)}) collective-permute-start(bf16[192,2048]{1,0:T(8,128)(2,1)} %get-tuple-element.14), channel_id=1, source_target_pairs={{0,1},{1,2},{2,3},{4,5},{5,6},{6,7},{8,9},{9,10},{10,11},{12,13},{... | collective-permute-start | bytes 2359304 | tf_op jit(solution)/shard_map/ppermute | solution.py:74
  143.2 28.5 %collective-permute-start.8 = (bf16[192,2048]{1,0:T(8,128)(2,1)}, bf16[192,2048]{1,0:T(8,128)(2,1)}, u32[]{:S(2)}, u32[]{:S(2)}) collective-permute-start(bf16[192,2048]{1,0:T(8,128)(2,1)} %add_convert_fusion.1), channel_id=1, source_target_pairs={{1,0},{2,1},{3,2},{5,4},{6,5},{7,6},{9,8},{10,9},{11,10},{13,12},{... | collective-permute-start | bytes 2359304 | tf_op jit(solution)/shard_map/ppermute | solution.py:75
  166.9 33.0 %collective-permute-start.10 = (f32[133,2048]{1,0:T(8,128)}, f32[133,2048]{1,0:T(8,128)}, u32[]{:S(2)}, u32[]{:S(2)}) collective-permute-start(f32[133,2048]{1,0:T(8,128)} %slice.157), channel_id=1, source_target_pairs={{4,0},{8,4},{12,8},{16,12},{20,16},{24,20},{28,24},{5,1},{9,5},{13... | collective-permute-start | bytes 3268616 | tf_op jit(solution)/shard_map/ppermute | solution.py:135
  169.6 29.0 %collective-permute-start.9 = (f32[6,2048]{1,0:T(8,128)S(1)}, f32[6,2048]{1,0:T(8,128)S(1)}, u32[]{:S(2)}, u32[]{:S(2)}) collective-permute-start(f32[6,2048]{1,0:T(8,128)S(1)} %slice.156), channel_id=1, source_target_pairs={{4,0},{8,4},{12,8},{16,12},{20,16},{24,20},{28,24},{5,1},{9,5},{13... | collective-permute-start | bytes 147464 | tf_op jit(solution)/shard_map/ppermute | solution.py:135
  203.0 13.4 %copy-start.3 = (f32[198,2048]{1,0:T(8,128)S(1)}, f32[198,2048]{1,0:T(8,128)}, u32[]{:S(2)}) copy-start(f32[198,2048]{1,0:T(8,128)} %get-tuple-element.8) | copy-start | bytes 4866052
  203.0 13.4 %copy-start.4 = (f32[198,2048]{1,0:T(8,128)S(1)}, f32[198,2048]{1,0:T(8,128)}, u32[]{:S(2)}) copy-start(f32[198,2048]{1,0:T(8,128)} %get-tuple-element.9) | copy-start | bytes 4866052
  216.5 1.9 copy-start.2
Sparse Core Ops, SparseCore 0:
  29.2 79.1 all-gather.1

commit v3 on v0

--- a/solution.py
+++ b/solution.py
@@ -58,6 +58,25 @@
     return [(j + 1, j) for j in range(n - 1)]
 
 
+def tp_all_gather(x, axis_name):
+    n = lax.axis_size(axis_name)
+    if n > 8:
+        return lax.all_gather(x, axis_name, axis=1, tiled=True)
+    k = lax.axis_index(axis_name)
+    width = x.shape[1]
+    right = x
+    left = x
+    got_r = []
+    got_l = []
+    for s in range(1, n):
+        right = lax.ppermute(right, axis_name, [(j, j + 1) for j in range(s - 1, n - 1)])
+        left = lax.ppermute(left, axis_name, [(j + 1, j) for j in range(0, n - s)])
+        got_r.append(right)
+        got_l.append(left)
+    stacked = jnp.concatenate(got_r[::-1] + [x] + got_l, axis=1)
+    return lax.dynamic_slice_in_dim(stacked, (n - 1 - k) * width, n * width, axis=1)
+
+
 def block(projected, feat_taps, filters, out_weight, cotangent):
     rows = projected.shape[0]
     feat_len = feat_taps.shape[0]
@@ -108,7 +127,7 @@
     query, key_ext, value_ext, conv = lax.optimization_barrier(
         (query, key_ext, value_ext, conv)
     )
-    cot_full = lax.all_gather(cotangent, "tp", axis=1, tiled=True)
+    cot_full = tp_all_gather(cotangent, "tp")
     grad_mixed = jnp.einsum(
         "te,ce->tc", cot_full, out_weight, preferred_element_type=jnp.float32
     )

time: 149 us -> 216 us (1.45)
  the two profiles are of different devices: /device:TPU:0 before, /device:TPU:3 now
where the time goes in v3:
time: 216 us; the launch traced here: 215 us
  waiting for transfers between devices  65.9 us (31%)
  matrix products  35.8 us (17%)
  Pallas kernels  26.7 us (12%)
  starting transfers between devices  25.5 us (12%)
  other arithmetic  25.2 us (12%)
  local copies, waits for them, and re-layouts  21.5 us (10%)
  between operations  14.3 us (7%)
    ppermute x3, waiting for transfers between devices, tp_all_gather(): left = lax.ppermute(left, axis_name, [(j + 1, j) for j in range(0, n - s)])  43.9 us
    pallas_call x2, Pallas kernels, toeplitz_conv(): pl.pallas_call(_toeplitz_kernel, grid=(steps,), in_specs=[pl.BlockSpec((g...  26.7 us
    dot_general x1, matrix products, block(): jnp.einsum('te,ce->tc', cot_full, out_weight, preferred_element_type=jnp....  19.2 us
    dot_general x1, matrix products, block(): jnp.einsum('tc,cd->td', mixed, out_weight, preferred_element_type=jnp.flo...  16.6 us
    ppermute x2, waiting for transfers between devices, block(): lax.ppermute((signal_grad[:reach], query_grad[:fh]), 'seq', bwd)  12.8 us
    unnamed x16, local copies, waits for them, and re-layouts  11.8 us
    ppermute x3, waiting for transfers between devices, tp_all_gather(): lax.ppermute(right, axis_name, [(j, j + 1) for j in range(s - 1, n - 1)])  9.24 us
    ppermute x3, starting transfers between devices, tp_all_gather(): lax.ppermute(right, axis_name, [(j, j + 1) for j in range(s - 1, n - 1)])  6.36 us
  transfers between devices with their start and end apart: 12, of which 4 were waited for; matrix products, arithmetic and copies ran while one was open for 33% of the time, Pallas kernels for 12%

profile of v3, /device:TPU:3, one launch (start us, length us, event | category | flops | bytes accessed | tf_op | source)
XLA Modules:
  0.0 215.0 jit_solution(8130192075198053422)
XLA Ops:
  8.2 2.6 %collective-permute-start.1 = (bf16[6,3,2048]{2,0,1:T(8,128)(2,1)S(1)}, bf16[6,3,2048]{2,0,1:T(8,128)(2,1)S(1)}, u32[]{:S(2)}, u32[]{:S(2)}) collective-permute-start(bf16[6,3,2048]{2,0,1:T(8,128)(2,1)S(1)} %get-tuple-element.15), channel_id=1, source_target_pairs={{4,0},{8,4},{12,8},{16,12},{20,16},{24,20},{28,24},{5,1},{9,5},{13... | collective-permute-start | bytes 221192 | tf_op jit(solution)/shard_map/ppermute | solution.py:103
  10.8 3.9 %collective-permute-start = (bf16[6,3,2048]{2,0,1:T(8,128)(2,1)S(1)}, bf16[6,3,2048]{2,0,1:T(8,128)(2,1)S(1)}, u32[]{:S(2)}, u32[]{:S(2)}) collective-permute-start(bf16[6,3,2048]{2,0,1:T(8,128)(2,1)S(1)} %get-tuple-element.14), channel_id=1, source_target_pairs={{0,4},{4,8},{8,12},{12,16},{16,20},{20,24},{24,28},{1,5},{5,9},{9,... | collective-permute-start | bytes 221192 | tf_op jit(solution)/shard_map/ppermute | solution.py:102
  14.7 1.8 fusion.18
  16.6 2.5 %maximum_convert_fusion = f32[204,3,2048]{2,0,1:T(8,128)S(1)} fusion(bf16[6,3,2048]{2,0,1:T(8,128)(2,1)S(1)} %collective-permute-done.1, bf16[192,3,2048]{2,0,1:T(8,128)(2,1)} %param.5, bf16[6,3,2048]{2,0,1:T(8,128)(2,1)S(1)} %collective-permute-done), kind=kLoop, calls=%fused_computation.33 | loop fusion | flops 7520256 | bytes 7520256 | tf_op jit(solution)/shard_map/convert_element_type | solution.py:104
  19.1 4.0 %fusion = f32[198,3,2048]{2,0,1:T(8,128)S(1)} fusion(f32[204,3,2048]{2,0,1:T(8,128)S(1)} %maximum_convert_fusion, f32[3,2048]{1,0:T(4,128)S(1)} %get-tuple-element.27, f32[3,2048]{1,0:T(4,128)S(1)} %get-tuple-element.28, f32[3,2048]{1,0:T(4,128)S(1)} %get-tuple-element.29, f32[3,2048]{1,0:T(4,128)S(1)} %get-tuple-element.30, ...), kind=kLoop, calls=%fused_computation.2 | loop fusion | flops 15814656 | bytes 39100416 | tf_op jit(solution)/shard_map/add | solution.py:107
  23.2 1.8 slice_bitcast_fusion.2
  24.9 1.3 slice_bitcast_fusion.3
  26.2 4.8 %collective-permute-start.2 = (f32[127,2048]{1,0:T(8,128)}, f32[127,2048]{1,0:T(8,128)}, u32[]{:S(2)}, u32[]{:S(2)}) collective-permute-start(f32[127,2048]{1,0:T(8,128)} %slice_bitcast_fusion.3), channel_id=1, source_target_pairs={{0,4},{4,8},{8,12},{12,16},{16,20},{20,24},{24,28},{1,5},{5,9},{9,... | collective-permute-start | bytes 3121160 | tf_op jit(solution)/shard_map/ppermute | solution.py:115
  31.1 4.1 %collective-permute-start.3 = (bf16[192,2048]{1,0:T(8,128)(2,1)}, bf16[192,2048]{1,0:T(8,128)(2,1)}, u32[]{:S(2)}, u32[]{:S(2)}) collective-permute-start(bf16[192,2048]{1,0:T(8,128)(2,1)} %param.9), channel_id=1, source_target_pairs={{0,1},{1,2},{2,3},{4,5},{5,6},{6,7},{8,9},{9,10},{10,11},{12,13},{... | collective-permute-start | bytes 2359304 | tf_op jit(solution)/shard_map/ppermute | solution.py:72
  37.3 3.4 %slice_bitcast_fusion = (f32[198,2048]{1,0:T(8,128)S(1)}, f32[198,2048]{1,0:T(8,128)}) fusion(f32[198,3,2048]{2,0,1:T(8,128)} %copy-done), kind=kLoop, calls=%fused_computation.34 | loop fusion | bytes 6488064 | tf_op jit(solution)/shard_map/squeeze | solution.py:110
  40.7 9.2 %collective-permute-done.3 = bf16[192,2048]{1,0:T(8,128)(2,1)} collective-permute-done((bf16[192,2048]{1,0:T(8,128)(2,1)}, bf16[192,2048]{1,0:T(8,128)(2,1)}, u32[]{:S(2)}, u32[]{:S(2)}) %collective-permute-start.3) | collective-permute-done | bytes 786464 | tf_op jit(solution)/shard_map/ppermute | solution.py:72
  50.0 1.5 collective-permute-start.4
  51.5 3.4 %collective-permute-done.6 = bf16[192,2048]{1,0:T(8,128)(2,1)} collective-permute-done((bf16[192,2048]{1,0:T(8,128)(2,1)}, bf16[192,2048]{1,0:T(8,128)(2,1)}, u32[]{:S(2)}, u32[]{:S(2)}) %collective-permute-start.6) | collective-permute-done | bytes 786464 | tf_op jit(solution)/shard_map/ppermute | solution.py:73
  56.3 3.2 %maximum_maximum_fusion.ext_ref = f32[384,2048]{1,0:T(8,128)} fusion(f32[192,2048]{1,0:T(8,128)S(1)} %bitcast.35, f32[127,2048]{1,0:T(8,128)} %collective-permute-done.2, f32[384]{0:T(512)S(1)} %pad.21.clone), kind=kLoop, calls=%fused_computation.29 | loop fusion | flops 1572864 | bytes 5760512 | tf_op jit(solution)/shard_map/concatenate | solution.py:116
  59.4 13.4 %shard_map.68 = f32[192,2048]{1,0:T(8,128)} custom-call(f32[128,256]{1,0:T(8,128)} %pad_convert_fusion.1.base_ref, f32[384,2048]{1,0:T(8,128)} %maximum_maximum_fusion.ext_ref), custom_call_target="tpu_custom_call" | custom-call | flops 3221225472 | bytes 4849664 | tf_op jit(solution)/shard_map/pallas_call | solution.py:40
  73.6 16.6 %convolution_convert_fusion = bf16[192,8192]{1,0:T(8,128)(2,1)} fusion(bf16[2048,8192]{1,0:T(8,128)(2,1)} %param.8, f32[192,2048]{1,0:T(8,128)} %shard_map.68, f32[198,3,2048]{2,0,1:T(8,128)} %copy-done), kind=kOutput, calls=%fused_computation | convolution fusion | flops 6444810240 | bytes 39845888 | tf_op jit(solution)/shard_map/tc,cd->td/dot_general | solution.py:122
  90.2 1.3 collective-permute-start.8
  92.5 2.1 constant_dynamic-update-slice_fusion.5
  94.6 2.1 constant_dynamic-update-slice_fusion.4
  96.7 2.1 constant_dynamic-update-slice_fusion.3
  98.8 2.3 %constant_dynamic-update-slice_fusion.2 = bf16[192,14336]{1,0:T(8,128)(2,1)} fusion(bf16[192,14336]{1,0:T(8,128)(2,1)} %constant_dynamic-update-slice_fusion.3, bf16[192,2048]{1,0:T(8,128)(2,1)} %collective-permute-done.6), kind=kLoop, calls=%fused_computation.54 | loop fusion | bytes 1572864
  101.1 2.1 constant_dynamic-update-slice_fusion.1
  103.3 40.4 %collective-permute-done.8 = bf16[192,2048]{1,0:T(8,128)(2,1)S(1)} collective-permute-done((bf16[192,2048]{1,0:T(8,128)(2,1)}, bf16[192,2048]{1,0:T(8,128)(2,1)S(1)}, u32[]{:S(2)}, u32[]{:S(2)}) %collective-permute-start.8) | collective-permute-done | bytes 786464 | tf_op jit(solution)/shard_map/ppermute | solution.py:73
  144.7 19.2 %fusion.17 = (f32[192,2048]{1,0:T(8,128)}, f32[192,2048]{1,0:T(8,128)S(1)}) fusion(f32[192,2048]{1,0:T(8,128)} %shard_map.68, f32[192,2048]{1,0:T(8,128)} %get-tuple-element.7, bf16[2048,8192]{1,0:T(8,128)(2,1)} %param.8, bf16[192,14336]{1,0:T(8,128)(2,1)} %constant_dynamic-update-slice_fusion, s32[]{:T(128)S(6)} %select_n.3), kind=kOutput, calls=%fused_computation.61 | convolution fusion | flops 6443237376 | bytes 42991620 | tf_op jit(solution)/shard_map/te,ce->tc/dot_general | solution.py:131
  163.9 1.9 collective-permute-start.10
  166.7 2.1 collective-permute-start.9
  169.6 12.8 %collective-permute-done.9 = f32[6,2048]{1,0:T(8,128)S(1)} collective-permute-done((f32[6,2048]{1,0:T(8,128)S(1)}, f32[6,2048]{1,0:T(8,128)S(1)}, u32[]{:S(2)}, u32[]{:S(2)}) %collective-permute-start.9) | collective-permute-done | bytes 49184 | tf_op jit(solution)/shard_map/ppermute | solution.py:136
  182.3 1.5 maximum_bitcast_fusion
  183.9 3.3 %maximum_maximum_fusion.1.ext_ref = f32[384,2048]{1,0:T(8,128)} fusion(f32[133,2048]{1,0:T(8,128)S(1)} %collective-permute-done.10, f32[192,2048]{1,0:T(8,128)} %copy-done.1, f32[384]{0:T(512)S(1)} %pad.16.clone), kind=kLoop, calls=%fused_computation.30 | loop fusion | flops 1572864 | bytes 5809664 | tf_op jit(solution)/shard_map/concatenate | solution.py:137
  187.2 13.3 %shard_map.69 = f32[224,2048]{1,0:T(8,128)} custom-call(f32[128,256]{1,0:T(8,128)} %pad_convert_fusion.base_ref, f32[384,2048]{1,0:T(8,128)} %maximum_maximum_fusion.1.ext_ref), custom_call_target="tpu_custom_call" | custom-call | flops 3758096384 | bytes 5111808 | tf_op jit(solution)/shard_map/pallas_call | solution.py:40
  200.5 2.3 %multiply_bitcast_fusion.1 = (f32[198,1,2048]{2,0,1:T(8,128)S(1)}, f32[198,1,2048]{2,0,1:T(8,128)S(1)}) fusion(f32[198,2048]{1,0:T(8,128)S(1)} %get-tuple-element.8, f32[224,2048]{1,0:T(8,128)} %shard_map.69, f32[198,2048]{1,0:T(8,128)} %get-tuple-element.9), kind=kLoop, calls=%fused_computation.38 | loop fusion | flops 811008 | bytes 8110080 | tf_op jit(solution)/shard_map/stack | solution.py:142
  203.2 5.0 %fusion.7 = bf16[192,3,2048]{2,0,1:T(8,128)(2,1)} fusion(f32[198,3,2048]{2,0,1:T(8,128)S(1)} %pad_maximum_fusion, f32[3,2048]{1,0:T(4,128)S(1)} %get-tuple-element.27, f32[3,2048]{1,0:T(4,128)S(1)} %get-tuple-element.28, f32[3,2048]{1,0:T(4,128)S(1)} %get-tuple-element.29, f32[3,2048]{1,0:T(4,128)S(1)} %get-tuple-element.30, ...), kind=kLoop, calls=%fused_computation.17 | loop fusion | flops 16515072 | bytes 35561472 | tf_op jit(solution)/shard_map/convert_element_type | solution.py:146
  (37 shorter events, 9.2 us)
Async XLA Ops:
  7.2 201.0 %reduce-scatter.2.cloned.1.call-start = ((), (), s32[]{:S(2)}) async-start(), calls=%async_computation.1 | async-start | bytes 3932160 | tf_op jit(solution)/shard_map/reduce_scatter | solution.py:125
  8.2 8.4 %collective-permute-start.1 = (bf16[6,3,2048]{2,0,1:T(8,128)(2,1)S(1)}, bf16[6,3,2048]{2,0,1:T(8,128)(2,1)S(1)}, u32[]{:S(2)}, u32[]{:S(2)}) collective-permute-start(bf16[6,3,2048]{2,0,1:T(8,128)(2,1)S(1)} %get-tuple-element.15), channel_id=1, source_target_pairs={{4,0},{8,4},{12,8},{16,12},{20,16},{24,20},{28,24},{5,1},{9,5},{13... | collective-permute-start | bytes 221192 | tf_op jit(solution)/shard_map/ppermute | solution.py:103
  10.8 5.9 %collective-permute-start = (bf16[6,3,2048]{2,0,1:T(8,128)(2,1)S(1)}, bf16[6,3,2048]{2,0,1:T(8,128)(2,1)S(1)}, u32[]{:S(2)}, u32[]{:S(2)}) collective-permute-start(bf16[6,3,2048]{2,0,1:T(8,128)(2,1)S(1)} %get-tuple-element.14), channel_id=1, source_target_pairs={{0,4},{4,8},{8,12},{12,16},{16,20},{20,24},{24,28},{1,5},{5,9},{9,... | collective-permute-start | bytes 221192 | tf_op jit(solution)/shard_map/ppermute | solution.py:102
  23.1 3.1 %copy-start = (f32[198,3,2048]{2,0,1:T(8,128)}, f32[198,3,2048]{2,0,1:T(8,128)S(1)}, u32[]{:S(2)}) copy-start(f32[198,3,2048]{2,0,1:T(8,128)S(1)} %fusion) | copy-start | bytes 14598148
  23.1 13.3 %copy-start.2 = (f32[128,128]{1,0:T(8,128)S(1)}, f32[128,128]{1,0:T(8,128)}, u32[]{:S(2)}) copy-start(f32[128,128]{1,0:T(8,128)} %param.7) | copy-start | bytes 196612
  26.2 30.0 %collective-permute-start.2 = (f32[127,2048]{1,0:T(8,128)}, f32[127,2048]{1,0:T(8,128)}, u32[]{:S(2)}, u32[]{:S(2)}) collective-permute-start(f32[127,2048]{1,0:T(8,128)} %slice_bitcast_fusion.3), channel_id=1, source_target_pairs={{0,4},{4,8},{8,12},{12,16},{16,20},{20,24},{24,28},{1,5},{5,9},{9,... | collective-permute-start | bytes 3121160 | tf_op jit(solution)/shard_map/ppermute | solution.py:115
  31.1 18.9 %collective-permute-start.3 = (bf16[192,2048]{1,0:T(8,128)(2,1)}, bf16[192,2048]{1,0:T(8,128)(2,1)}, u32[]{:S(2)}, u32[]{:S(2)}) collective-permute-start(bf16[192,2048]{1,0:T(8,128)(2,1)} %param.9), channel_id=1, source_target_pairs={{0,1},{1,2},{2,3},{4,5},{5,6},{6,7},{8,9},{9,10},{10,11},{12,13},{... | collective-permute-start | bytes 2359304 | tf_op jit(solution)/shard_map/ppermute | solution.py:72
  35.2 19.8 %collective-permute-start.6 = (bf16[192,2048]{1,0:T(8,128)(2,1)}, bf16[192,2048]{1,0:T(8,128)(2,1)}, u32[]{:S(2)}, u32[]{:S(2)}) collective-permute-start(bf16[192,2048]{1,0:T(8,128)(2,1)} %param.9), channel_id=1, source_target_pairs={{1,0},{2,1},{3,2},{5,4},{6,5},{7,6},{9,8},{10,9},{11,10},{13,12},{... | collective-permute-start | bytes 2359304 | tf_op jit(solution)/shard_map/ppermute | solution.py:73
  50.0 22.9 %collective-permute-start.4 = (bf16[192,2048]{1,0:T(8,128)(2,1)}, bf16[192,2048]{1,0:T(8,128)(2,1)}, u32[]{:S(2)}, u32[]{:S(2)}) collective-permute-start(bf16[192,2048]{1,0:T(8,128)(2,1)} %collective-permute-done.3), channel_id=1, source_target_pairs={{1,2},{2,3},{5,6},{6,7},{9,10},{10,11},{13,14},{14,15},{17,18},{18... | collective-permute-start | bytes 2359304 | tf_op jit(solution)/shard_map/ppermute | solution.py:72
  55.0 35.3 %collective-permute-start.7 = (bf16[192,2048]{1,0:T(8,128)(2,1)}, bf16[192,2048]{1,0:T(8,128)(2,1)}, u32[]{:S(2)}, u32[]{:S(2)}) collective-permute-start(bf16[192,2048]{1,0:T(8,128)(2,1)} %collective-permute-done.6), channel_id=1, source_target_pairs={{1,0},{2,1},{5,4},{6,5},{9,8},{10,9},{13,12},{14,13},{17,16},{18,1... | collective-permute-start | bytes 2359304 | tf_op jit(solution)/shard_map/ppermute | solution.py:73
  72.9 18.7 %collective-permute-start.5 = (bf16[192,2048]{1,0:T(8,128)(2,1)}, bf16[192,2048]{1,0:T(8,128)(2,1)S(1)}, u32[]{:S(2)}, u32[]{:S(2)}) collective-permute-start(bf16[192,2048]{1,0:T(8,128)(2,1)} %collective-permute-done.4), channel_id=1, source_target_pairs={{2,3},{6,7},{10,11},{14,15},{18,19},{22,23},{26,27},{30,31}} | collective-permute-start | bytes 2359304 | tf_op jit(solution)/shard_map/ppermute | solution.py:72
  90.2 53.5 %collective-permute-start.8 = (bf16[192,2048]{1,0:T(8,128)(2,1)}, bf16[192,2048]{1,0:T(8,128)(2,1)S(1)}, u32[]{:S(2)}, u32[]{:S(2)}) collective-permute-start(bf16[192,2048]{1,0:T(8,128)(2,1)} %collective-permute-done.7), channel_id=1, source_target_pairs={{1,0},{5,4},{9,8},{13,12},{17,16},{21,20},{25,24},{29,28}} | collective-permute-start | bytes 2359304 | tf_op jit(solution)/shard_map/ppermute | solution.py:73
  163.8 5.7 %copy-start.1 = (f32[192,2048]{1,0:T(8,128)}, f32[192,2048]{1,0:T(8,128)S(1)}, u32[]{:S(2)}) copy-start(f32[192,2048]{1,0:T(8,128)S(1)} %get-tuple-element.19) | copy-start | bytes 4718596
  163.9 20.0 %collective-permute-start.10 = (f32[133,2048]{1,0:T(8,128)S(1)}, f32[133,2048]{1,0:T(8,128)S(1)}, u32[]{:S(2)}, u32[]{:S(2)}) collective-permute-start(f32[133,2048]{1,0:T(8,128)S(1)} %slice.157), channel_id=1, source_target_pairs={{4,0},{8,4},{12,8},{16,12},{20,16},{24,20},{28,24},{5,1},{9,5},{13... | collective-permute-start | bytes 3268616 | tf_op jit(solution)/shard_map/ppermute | solution.py:136
  166.7 15.6 %collective-permute-start.9 = (f32[6,2048]{1,0:T(8,128)S(1)}, f32[6,2048]{1,0:T(8,128)S(1)}, u32[]{:S(2)}, u32[]{:S(2)}) collective-permute-start(f32[6,2048]{1,0:T(8,128)S(1)} %slice.156), channel_id=1, source_target_pairs={{4,0},{8,4},{12,8},{16,12},{20,16},{24,20},{28,24},{5,1},{9,5},{13... | collective-permute-start | bytes 147464 | tf_op jit(solution)/shard_map/ppermute | solution.py:136
Sparse Core Ops, SparseCore 0:
  90.3 72.7 reduce-scatter.1

commit v4 on v0

--- a/solution.py
+++ b/solution.py
@@ -82,13 +82,18 @@
 
     prev_proj = lax.ppermute(projected[rows - fh:], "seq", fwd)
     next_proj = lax.ppermute(projected[:fh], "seq", bwd)
-    ext = jnp.concatenate([prev_proj, projected, next_proj], axis=0).astype(jnp.float32)
-    feats = feat_taps[0] * ext[fh:fh + rows + fh]
-    for d in range(1, feat_len):
-        feats = feats + feat_taps[d] * ext[fh - d:fh - d + rows + fh]
-    query = feats[:rows, 0]
-    key_ext = feats[:, 1]
-    value_ext = feats[:, 2]
+    ext = jnp.concatenate([prev_proj, projected, next_proj], axis=0)
+
+    def featurize(stream, out_rows):
+        sig = ext[:, stream].astype(jnp.float32)
+        out = feat_taps[0, stream] * sig[fh:fh + out_rows]
+        for d in range(1, feat_len):
+            out = out + feat_taps[d, stream] * sig[fh - d:fh - d + out_rows]
+        return out
+
+    query = featurize(0, rows)
+    key_ext = featurize(1, rows + fh)
+    value_ext = featurize(2, rows + fh)
     key_feat = key_ext[:rows]
     value_feat = value_ext[:rows]
     product = key_feat * value_feat

time: 149 us -> 150 us (level)
  local copies, waits for them, and re-layouts: 8.14 us -> 4.91 us
  other arithmetic: 22.9 us -> 25.6 us
    reduce_scatter x1, waiting for transfers between devices: 16.6 us -> 12.5 us  [block(): output = lax.psum_scatter(partial, 'tp', scatter_dimension=1, tiled=True)]
    all_gather x1, waiting for transfers between devices: 11.9 us -> 15.8 us  [block(): cot_full = lax.all_gather(cotangent, 'tp', axis=1, tiled=True)]
    squeeze x1 -> x0, local copies, waits for them, and re-layouts: 3.45 us -> none  [block(): value_ext = feats[:, 2]]
    concatenate x0 -> x1, other arithmetic: none -> 2.44 us  [block(): ext = jnp.concatenate([prev_proj, projected, next_proj], axis=0)]
    convert_element_type x1, other arithmetic: 2.45 us -> 0.66 us  [featurize(): sig = ext[:, stream].astype(jnp.float32)]
    squeeze x1 -> x0, other arithmetic: 1.76 us -> none  [block(): query = feats[:rows, 0]]
    add x1 -> x3, other arithmetic: 4.03 us -> 5.07 us  [featurize(): out = out + feat_taps[d, stream] * sig[fh - d:fh - d + out_rows]]
where the time goes in v4:
time: 150 us; the launch traced here: 148 us
  matrix products  35 us (23%)
  waiting for transfers between devices  30.1 us (20%)
  Pallas kernels  26.8 us (18%)
  other arithmetic  25.6 us (17%)
  between operations  14.3 us (10%)
  starting transfers between devices  11.7 us (8%)
  local copies, waits for them, and re-layouts  4.91 us (3%)
    pallas_call x2, Pallas kernels, toeplitz_conv(): pl.pallas_call(_toeplitz_kernel, grid=(steps,), in_specs=[pl.BlockSpec((g...  26.8 us
    dot_general x1, matrix products, block(): jnp.einsum('te,ce->tc', cot_full, out_weight, preferred_element_type=jnp....  18.2 us
    dot_general x1, matrix products, block(): jnp.einsum('tc,cd->td', mixed, out_weight, preferred_element_type=jnp.flo...  16.8 us
    all_gather x1, waiting for transfers between devices, block(): cot_full = lax.all_gather(cotangent, 'tp', axis=1, tiled=True)  15.8 us
    reduce_scatter x1, waiting for transfers between devices, block(): output = lax.psum_scatter(partial, 'tp', scatter_dimension=1, tiled=True)  12.5 us
    add x3, other arithmetic, featurize(): out = out + feat_taps[d, stream] * sig[fh - d:fh - d + out_rows]  5.07 us
    convert_element_type x1, other arithmetic, block(): return (output, igrad.astype(jnp.bfloat16))  4.96 us
    ppermute x1, starting transfers between devices, block(): prev_prod = lax.ppermute(product[rows - lh:], 'seq', fwd)  4.73 us
  transfers between devices with their start and end apart: 7, of which 3 were waited for; matrix products, arithmetic and copies ran while one was open for 43% of the time, Pallas kernels for 18%

profile of v4, /device:TPU:0, one launch (start us, length us, event | category | flops | bytes accessed | tf_op | source)
XLA Modules:
  0.0 148.4 jit_solution(16377578491371402292)
XLA Ops:
  7.2 1.0 fusion.46
  8.2 1.3 collective-permute-start.1
  9.5 3.0 %collective-permute-start = (bf16[6,3,2048]{2,0,1:T(8,128)(2,1)S(1)}, bf16[6,3,2048]{2,0,1:T(8,128)(2,1)S(1)}, u32[]{:S(2)}, u32[]{:S(2)}) collective-permute-start(bf16[6,3,2048]{2,0,1:T(8,128)(2,1)S(1)} %get-tuple-element.13), channel_id=1, source_target_pairs={{0,4},{4,8},{8,12},{12,16},{16,20},{20,24},{24,28},{1,5},{5,9},{9,... | collective-permute-start | bytes 221192 | tf_op jit(solution)/shard_map/ppermute | solution.py:83
  12.6 0.9 rev.3
  13.6 1.5 convert.9
  15.0 1.7 %fusion.49 = (f32[1,1,2048]{2,0,1:T(1,128)S(1)}, f32[1,1,2048]{2,0,1:T(1,128)S(1)}, f32[1,1,2048]{2,0,1:T(1,128)S(1)}, f32[1,1,2048]{2,0,1:T(1,128)S(1)}, f32[1,...) fusion(f32[7,3,2048]{2,0,1:T(8,128)} %param.6), kind=kLoop, calls=%fused_computation.99 | loop fusion | bytes 311296 | tf_op jit(solution)/shard_map/slice | solution.py:89
  16.8 0.8 fusion.48
  17.7 0.7 pad_convert_fusion.1.base_ref
  18.3 2.4 %pad_maximum_fusion.1 = bf16[204,3,2048]{2,0,1:T(8,128)(2,1)S(1)} fusion(bf16[6,3,2048]{2,0,1:T(8,128)(2,1)S(1)} %collective-permute-done.1, bf16[192,3,2048]{2,0,1:T(8,128)(2,1)} %param.5, bf16[6,3,2048]{2,0,1:T(8,128)(2,1)S(1)} %collective-permute-done), kind=kLoop, calls=%fused_computation.18 | loop fusion | flops 7520256 | bytes 5013504 | tf_op jit(solution)/shard_map/concatenate | solution.py:85
  20.8 0.7 slice_convert_fusion.1
  21.4 1.3 fusion.8
  22.8 1.3 fusion.21
  24.1 0.2 slice_multiply_fusion.7
  24.4 4.7 %collective-permute-start.2 = (f32[127,2048]{1,0:T(8,128)S(1)}, f32[127,2048]{1,0:T(8,128)S(1)}, u32[]{:S(2)}, u32[]{:S(2)}) collective-permute-start(f32[127,2048]{1,0:T(8,128)S(1)} %slice.378), channel_id=1, source_target_pairs={{0,4},{4,8},{8,12},{12,16},{16,20},{20,24},{24,28},{1,5},{5,9},{9,... | collective-permute-start | bytes 3121160 | tf_op jit(solution)/shard_map/ppermute | solution.py:101
  29.1 2.4 %fusion.34 = f32[192,2048]{1,0:T(8,128)} fusion(f32[204,1,2048]{2,0,1:T(8,128)S(1)} %get-tuple-element.12, f32[2048]{0:T(1024)S(1)} %bitcast.202, f32[2048]{0:T(1024)S(1)} %bitcast.203, f32[2048]{0:T(1024)S(1)} %bitcast.204, f32[2048]{0:T(1024)S(1)} %bitcast.205, f32[2048]{0:T(1024)S(1)} %bitcast.206, f32[2048]{0:T(1024)S(1)} %bitcast.222, f32[2048]{0:T(1024)S(1)} %bitcast.221), kind=kLoop, calls=%fused_computation.65 | loop fusion | flops 5111808 | bytes 12640256 | tf_op jit(solution)/shard_map/add | solution.py:91
  31.6 2.0 %maximum_maximum_fusion.ext_ref = f32[384,2048]{1,0:T(8,128)} fusion(f32[192,2048]{1,0:T(8,128)S(1)} %slice_multiply_fusion.7, f32[127,2048]{1,0:T(8,128)S(1)} %collective-permute-done.2, f32[384]{0:T(512)S(1)} %pad.21.clone), kind=kLoop, calls=%fused_computation.16 | loop fusion | flops 1572864 | bytes 5760512 | tf_op jit(solution)/shard_map/concatenate | solution.py:102
  33.5 13.4 %shard_map.68 = f32[192,2048]{1,0:T(8,128)} custom-call(f32[128,256]{1,0:T(8,128)} %pad_convert_fusion.1.base_ref, f32[384,2048]{1,0:T(8,128)} %maximum_maximum_fusion.ext_ref), custom_call_target="tpu_custom_call" | custom-call | flops 3221225472 | bytes 4849664 | tf_op jit(solution)/shard_map/pallas_call | solution.py:40
  47.0 16.8 %convolution_convert_fusion = bf16[192,8192]{1,0:T(8,128)(2,1)} fusion(bf16[2048,8192]{1,0:T(8,128)(2,1)} %param.8, f32[192,2048]{1,0:T(8,128)} %fusion.34, f32[192,2048]{1,0:T(8,128)} %shard_map.68), kind=kOutput, calls=%fused_computation | convolution fusion | flops 6444810240 | bytes 39845888 | tf_op jit(solution)/shard_map/tc,cd->td/dot_general | solution.py:108
  63.8 15.8 %all-gather.2.cloned.1.call-done = bf16[192,8192]{1,0:T(8,128)(2,1)} async-done(((bf16[192,2048]{1,0:T(8,128)(2,1)}), bf16[192,8192]{1,0:T(8,128)(2,1)}) %all-gather.2.cloned.1.call-update) | async-done | bytes 3145744 | tf_op jit(solution)/shard_map/all_gather | solution.py:116
  79.6 18.2 %fusion.51 = f32[192,2048]{1,0:T(8,128)} fusion(bf16[192,8192]{1,0:T(8,128)(2,1)} %all-gather.2.cloned.1.call-done, bf16[2048,8192]{1,0:T(8,128)(2,1)} %param.8), kind=kOutput, calls=%fused_computation.101 | convolution fusion | flops 6442450944 | bytes 38273024 | tf_op jit(solution)/shard_map/te,ce->tc/dot_general | solution.py:117
  97.8 1.7 %fusion.47 = (f32[192,2048]{1,0:T(8,128)S(1)}, f32[192,2048]{1,0:T(8,128)S(1)}) fusion(f32[192,2048]{1,0:T(8,128)} %fusion.51, f32[192,2048]{1,0:T(8,128)S(1)} %copy-done.2, f32[192,2048]{1,0:T(8,128)S(1)} %copy-done.1), kind=kLoop, calls=%fused_computation.97 | loop fusion | flops 786432 | bytes 7864320 | tf_op jit(solution)/shard_map/mul | solution.py:121
  99.6 1.3 collective-permute-start.4
  101.1 1.3 collective-permute-start.3
  102.4 0.7 pad_convert_fusion.base_ref
  103.2 1.7 %collective-permute-done.3 = f32[6,2048]{1,0:T(8,128)S(1)} collective-permute-done((f32[6,2048]{1,0:T(8,128)S(1)}, f32[6,2048]{1,0:T(8,128)S(1)}, u32[]{:S(2)}, u32[]{:S(2)}) %collective-permute-start.3) | collective-permute-done | bytes 49184 | tf_op jit(solution)/shard_map/ppermute | solution.py:122
  104.8 1.3 maximum_bitcast_fusion
  106.2 1.9 %maximum_maximum_fusion.1.ext_ref = f32[384,2048]{1,0:T(8,128)} fusion(f32[133,2048]{1,0:T(8,128)S(1)} %collective-permute-done.4, f32[192,2048]{1,0:T(8,128)S(1)} %get-tuple-element.18, f32[384]{0:T(512)S(1)} %pad.16.clone), kind=kLoop, calls=%fused_computation.17 | loop fusion | flops 1572864 | bytes 5809664 | tf_op jit(solution)/shard_map/concatenate | solution.py:123
  108.1 13.3 %shard_map.69 = f32[224,2048]{1,0:T(8,128)} custom-call(f32[128,256]{1,0:T(8,128)} %pad_convert_fusion.base_ref, f32[384,2048]{1,0:T(8,128)} %maximum_maximum_fusion.1.ext_ref), custom_call_target="tpu_custom_call" | custom-call | flops 3758096384 | bytes 5111808 | tf_op jit(solution)/shard_map/pallas_call | solution.py:40
  121.4 2.0 %multiply_bitcast_fusion.1 = (f32[198,1,2048]{2,0,1:T(8,128)S(1)}, f32[198,1,2048]{2,0,1:T(8,128)S(1)}) fusion(f32[198,2048]{1,0:T(8,128)S(1)} %fusion.8, f32[224,2048]{1,0:T(8,128)} %shard_map.69, f32[198,2048]{1,0:T(8,128)S(1)} %fusion.21), kind=kLoop, calls=%fused_computation.61 | loop fusion | flops 811008 | bytes 8110080 | tf_op jit(solution)/shard_map/stack | solution.py:128
  123.4 0.6 pad_maximum_fusion
  124.0 5.0 %fusion.1 = bf16[192,3,2048]{2,0,1:T(8,128)(2,1)} fusion(f32[198,3,2048]{2,0,1:T(8,128)S(1)} %pad_maximum_fusion, f32[3,2048]{1,0:T(4,128)S(1)} %get-tuple-element.47, f32[3,2048]{1,0:T(4,128)S(1)} %get-tuple-element.48, f32[3,2048]{1,0:T(4,128)S(1)} %get-tuple-element.49, f32[3,2048]{1,0:T(4,128)S(1)} %get-tuple-element.50, ...), kind=kLoop, calls=%fused_computation.4 | loop fusion | flops 16515072 | bytes 35561472 | tf_op jit(solution)/shard_map/convert_element_type | solution.py:132
  129.0 12.5 %reduce-scatter.2.cloned.1.call-done = bf16[192,2048]{1,0:T(8,128)(2,1)} async-done(((bf16[192,8192]{1,0:T(8,128)(2,1)}), bf16[192,2048]{1,0:T(8,128)(2,1)}) %reduce-scatter.2.cloned.1.call-update) | async-done | bytes 786448 | tf_op jit(solution)/shard_map/reduce_scatter | solution.py:111
  (40 shorter events, 0.6 us)
Async XLA Ops:
  7.2 9.6 %copy-start.3 = (f32[7,3,2048]{2,0,1:T(8,128)S(1)}, f32[7,3,2048]{2,0,1:T(8,128)}, u32[]{:S(2)}) copy-start(f32[7,3,2048]{2,0,1:T(8,128)} %param.6) | copy-start | bytes 516100
  7.2 72.4 %all-gather.2.cloned.1.call-start = ((), (), s32[]{:S(2)}) async-start(), calls=%async_computation.2 | async-start | bytes 3932160 | tf_op jit(solution)/shard_map/all_gather | solution.py:116
  8.2 10.1 %collective-permute-start.1 = (bf16[6,3,2048]{2,0,1:T(8,128)(2,1)S(1)}, bf16[6,3,2048]{2,0,1:T(8,128)(2,1)S(1)}, u32[]{:S(2)}, u32[]{:S(2)}) collective-permute-start(bf16[6,3,2048]{2,0,1:T(8,128)(2,1)S(1)} %get-tuple-element.14), channel_id=1, source_target_pairs={{4,0},{8,4},{12,8},{16,12},{20,16},{24,20},{28,24},{5,1},{9,5},{13... | collective-permute-start | bytes 221192 | tf_op jit(solution)/shard_map/ppermute | solution.py:84
  9.5 8.8 %collective-permute-start = (bf16[6,3,2048]{2,0,1:T(8,128)(2,1)S(1)}, bf16[6,3,2048]{2,0,1:T(8,128)(2,1)S(1)}, u32[]{:S(2)}, u32[]{:S(2)}) collective-permute-start(bf16[6,3,2048]{2,0,1:T(8,128)(2,1)S(1)} %get-tuple-element.13), channel_id=1, source_target_pairs={{0,4},{4,8},{8,12},{12,16},{16,20},{20,24},{24,28},{1,5},{5,9},{9,... | collective-permute-start | bytes 221192 | tf_op jit(solution)/shard_map/ppermute | solution.py:83
  12.6 128.9 %reduce-scatter.2.cloned.1.call-start = ((), (), s32[]{:S(2)}) async-start(), calls=%async_computation.1 | async-start | bytes 3932160 | tf_op jit(solution)/shard_map/reduce_scatter | solution.py:111
  24.4 7.2 %collective-permute-start.2 = (f32[127,2048]{1,0:T(8,128)S(1)}, f32[127,2048]{1,0:T(8,128)S(1)}, u32[]{:S(2)}, u32[]{:S(2)}) collective-permute-start(f32[127,2048]{1,0:T(8,128)S(1)} %slice.378), channel_id=1, source_target_pairs={{0,4},{4,8},{8,12},{12,16},{16,20},{20,24},{24,28},{1,5},{5,9},{9,... | collective-permute-start | bytes 3121160 | tf_op jit(solution)/shard_map/ppermute | solution.py:101
  79.6 18.2 %copy-start.1 = (f32[192,2048]{1,0:T(8,128)S(1)}, f32[192,2048]{1,0:T(8,128)}, u32[]{:S(2)}) copy-start(f32[192,2048]{1,0:T(8,128)} %fusion.34) | copy-start | bytes 4718596
  79.6 18.2 %copy-start.2 = (f32[192,2048]{1,0:T(8,128)S(1)}, f32[192,2048]{1,0:T(8,128)}, u32[]{:S(2)}) copy-start(f32[192,2048]{1,0:T(8,128)} %shard_map.68) | copy-start | bytes 4718596
  99.5 1.4 copy-start.8
  99.5 1.4 copy-start.9
  99.5 1.5 copy-start.6
  99.5 1.5 copy-start.7
  99.5 2.8 %copy-start.4 = (bf16[128,128]{1,0:T(8,128)(2,1)S(1)}, bf16[128,128]{1,0:T(8,128)(2,1)}, u32[]{:S(2)}) copy-start(bf16[128,128]{1,0:T(8,128)(2,1)} %convert.9) | copy-start | bytes 98308
  99.6 3.6 %copy-start.5 = (f32[1,3,2048]{2,0,1:T(1,128)S(1)}, f32[1,3,2048]{2,0,1:T(1,128)}, u32[]{:S(2)}) copy-start(f32[1,3,2048]{2,0,1:T(1,128)} %get-tuple-element.19) | copy-start | bytes 73732
  99.6 6.5 %collective-permute-start.4 = (f32[133,2048]{1,0:T(8,128)S(1)}, f32[133,2048]{1,0:T(8,128)S(1)}, u32[]{:S(2)}, u32[]{:S(2)}) collective-permute-start(f32[133,2048]{1,0:T(8,128)S(1)} %slice.380), channel_id=1, source_target_pairs={{4,0},{8,4},{12,8},{16,12},{20,16},{24,20},{28,24},{5,1},{9,5},{13... | collective-permute-start | bytes 3268616 | tf_op jit(solution)/shard_map/ppermute | solution.py:122
  101.1 3.8 %collective-permute-start.3 = (f32[6,2048]{1,0:T(8,128)S(1)}, f32[6,2048]{1,0:T(8,128)S(1)}, u32[]{:S(2)}, u32[]{:S(2)}) collective-permute-start(f32[6,2048]{1,0:T(8,128)S(1)} %slice.379), channel_id=1, source_target_pairs={{4,0},{8,4},{12,8},{16,12},{20,16},{24,20},{28,24},{5,1},{9,5},{13... | collective-permute-start | bytes 147464 | tf_op jit(solution)/shard_map/ppermute | solution.py:122
  121.4 2.0 %copy-start = (f32[198,1,2048]{2,0,1:T(8,128)S(1)}, f32[198,1,2048]{2,0,1:T(8,128)}, u32[]{:S(2)}) copy-start(f32[198,1,2048]{2,0,1:T(8,128)} %maximum_bitcast_fusion) | copy-start | bytes 4866052
Sparse Core Ops, SparseCore 0:
  12.7 66.8 all-gather.1
  82.4 59.0 reduce-scatter.1

commit v5 on v4

--- a/solution.py
+++ b/solution.py
@@ -105,17 +105,19 @@
     conv = toeplitz_conv(base_fwd, pext, fwd_rows)
     mixed = (query * conv).astype(jnp.bfloat16)
 
+    n_tp = lax.axis_size("tp")
+    weight_blocks = out_weight.reshape(channels, n_tp, out_weight.shape[1] // n_tp)
     partial = jnp.einsum(
-        "tc,cd->td", mixed, out_weight, preferred_element_type=jnp.float32
+        "tc,cbd->btd", mixed, weight_blocks, preferred_element_type=jnp.float32
     ).astype(jnp.bfloat16)
-    output = lax.psum_scatter(partial, "tp", scatter_dimension=1, tiled=True)
+    output = lax.psum_scatter(partial, "tp", scatter_dimension=0, tiled=False)
 
     query, key_ext, value_ext, conv = lax.optimization_barrier(
         (query, key_ext, value_ext, conv)
     )
-    cot_full = lax.all_gather(cotangent, "tp", axis=1, tiled=True)
+    cot_blocks = lax.all_gather(cotangent, "tp", axis=0, tiled=False)
     grad_mixed = jnp.einsum(
-        "te,ce->tc", cot_full, out_weight, preferred_element_type=jnp.float32
+        "bte,cbe->tc", cot_blocks, weight_blocks, preferred_element_type=jnp.float32
     )
     signal_grad = grad_mixed * query
     query_grad = grad_mixed * conv

time: 150 us -> 151 us (level)
  waiting for transfers between devices: 30.1 us -> 27.8 us
    reduce_scatter x1, waiting for transfers between devices: 12.5 us -> 10.4 us  [block(): output = lax.psum_scatter(partial, 'tp', scatter_dimension=0, tiled=False)]
  transfers between devices with their start and end apart: 7 -> 7, of which waited for: 3 -> 3; matrix products, arithmetic and copies ran while one was open for 43% -> 45% of each run, Pallas kernels for 18% -> 18%
where the time goes in v5:
time: 151 us; the launch traced here: 148 us
  matrix products  35.9 us (24%)
  waiting for transfers between devices  27.8 us (18%)
  other arithmetic  26.8 us (18%)
  Pallas kernels  26.7 us (18%)
  between operations  14.3 us (9%)
  starting transfers between devices  11.9 us (8%)
  local copies, waits for them, and re-layouts  4.89 us (3%)
    pallas_call x2, Pallas kernels, toeplitz_conv(): pl.pallas_call(_toeplitz_kernel, grid=(steps,), in_specs=[pl.BlockSpec((g...  26.7 us
    dot_general x1, matrix products, block(): jnp.einsum('bte,cbe->tc', cot_blocks, weight_blocks, preferred_element_ty...  19.2 us
    dot_general x1, matrix products, block(): jnp.einsum('tc,cbd->btd', mixed, weight_blocks, preferred_element_type=jn...  16.8 us
    all_gather x1, waiting for transfers between devices, block(): cot_blocks = lax.all_gather(cotangent, 'tp', axis=0, tiled=False)  15.9 us
    reduce_scatter x1, waiting for transfers between devices, block(): output = lax.psum_scatter(partial, 'tp', scatter_dimension=0, tiled=False)  10.4 us
    add x3, other arithmetic, featurize(): out = out + feat_taps[d, stream] * sig[fh - d:fh - d + out_rows]  5.07 us
    convert_element_type x1, other arithmetic, block(): return (output, igrad.astype(jnp.bfloat16))  4.96 us
    ppermute x1, starting transfers between devices, block(): prev_prod = lax.ppermute(product[rows - lh:], 'seq', fwd)  4.73 us
  transfers between devices with their start and end apart: 7, of which 3 were waited for; matrix products, arithmetic and copies ran while one was open for 45% of the time, Pallas kernels for 18%

profile of v5, /device:TPU:0, one launch (start us, length us, event | category | flops | bytes accessed | tf_op | source)
XLA Modules:
  0.0 148.4 jit_solution(8893549345331920894)
XLA Ops:
  7.2 1.0 fusion.63
  8.2 1.3 collective-permute-start.1
  9.5 3.0 %collective-permute-start = (bf16[6,3,2048]{2,0,1:T(8,128)(2,1)S(1)}, bf16[6,3,2048]{2,0,1:T(8,128)(2,1)S(1)}, u32[]{:S(2)}, u32[]{:S(2)}) collective-permute-start(bf16[6,3,2048]{2,0,1:T(8,128)(2,1)S(1)} %get-tuple-element.13), channel_id=1, source_target_pairs={{0,4},{4,8},{8,12},{12,16},{16,20},{20,24},{24,28},{1,5},{5,9},{9,... | collective-permute-start | bytes 221192 | tf_op jit(solution)/shard_map/ppermute | solution.py:83
  12.6 0.9 rev.3
  13.6 1.5 convert.9
  15.0 1.7 %fusion.66 = (f32[1,1,2048]{2,0,1:T(1,128)S(1)}, f32[1,1,2048]{2,0,1:T(1,128)S(1)}, f32[1,1,2048]{2,0,1:T(1,128)S(1)}, f32[1,1,2048]{2,0,1:T(1,128)S(1)}, f32[1,...) fusion(f32[7,3,2048]{2,0,1:T(8,128)} %param.6), kind=kLoop, calls=%fused_computation.108 | loop fusion | bytes 311296 | tf_op jit(solution)/shard_map/slice | solution.py:89
  16.8 0.8 fusion.65
  17.6 0.7 pad_convert_fusion.1.base_ref
  18.3 2.4 %pad_maximum_fusion.1 = bf16[204,3,2048]{2,0,1:T(8,128)(2,1)S(1)} fusion(bf16[6,3,2048]{2,0,1:T(8,128)(2,1)S(1)} %collective-permute-done.1, bf16[192,3,2048]{2,0,1:T(8,128)(2,1)} %param.5, bf16[6,3,2048]{2,0,1:T(8,128)(2,1)S(1)} %collective-permute-done), kind=kLoop, calls=%fused_computation.26 | loop fusion | flops 7520256 | bytes 5013504 | tf_op jit(solution)/shard_map/concatenate | solution.py:85
  20.8 0.7 slice_convert_fusion.1
  21.4 1.3 fusion.23
  22.8 1.3 fusion.36
  24.1 0.2 slice_multiply_fusion.7
  24.4 4.7 %collective-permute-start.2 = (f32[127,2048]{1,0:T(8,128)S(1)}, f32[127,2048]{1,0:T(8,128)S(1)}, u32[]{:S(2)}, u32[]{:S(2)}) collective-permute-start(f32[127,2048]{1,0:T(8,128)S(1)} %slice.378), channel_id=1, source_target_pairs={{0,4},{4,8},{8,12},{12,16},{16,20},{20,24},{24,28},{1,5},{5,9},{9,... | collective-permute-start | bytes 3121160 | tf_op jit(solution)/shard_map/ppermute | solution.py:101
  29.1 2.4 %fusion.49 = f32[192,2048]{1,0:T(8,128)} fusion(f32[204,1,2048]{2,0,1:T(8,128)S(1)} %get-tuple-element.12, f32[2048]{0:T(1024)S(1)} %bitcast.221, f32[2048]{0:T(1024)S(1)} %bitcast.222, f32[2048]{0:T(1024)S(1)} %bitcast.223, f32[2048]{0:T(1024)S(1)} %bitcast.224, f32[2048]{0:T(1024)S(1)} %bitcast.225, f32[2048]{0:T(1024)S(1)} %bitcast.241, f32[2048]{0:T(1024)S(1)} %bitcast.240), kind=kLoop, calls=%fused_computation.73 | loop fusion | flops 5111808 | bytes 12640256 | tf_op jit(solution)/shard_map/add | solution.py:91
  31.6 1.9 %maximum_maximum_fusion.ext_ref = f32[384,2048]{1,0:T(8,128)} fusion(f32[192,2048]{1,0:T(8,128)S(1)} %slice_multiply_fusion.7, f32[127,2048]{1,0:T(8,128)S(1)} %collective-permute-done.2, f32[384]{0:T(512)S(1)} %pad.21.clone), kind=kLoop, calls=%fused_computation.22 | loop fusion | flops 1572864 | bytes 5760512 | tf_op jit(solution)/shard_map/concatenate | solution.py:102
  33.5 13.4 %shard_map.68 = f32[192,2048]{1,0:T(8,128)} custom-call(f32[128,256]{1,0:T(8,128)} %pad_convert_fusion.1.base_ref, f32[384,2048]{1,0:T(8,128)} %maximum_maximum_fusion.ext_ref), custom_call_target="tpu_custom_call" | custom-call | flops 3221225472 | bytes 4849664 | tf_op jit(solution)/shard_map/pallas_call | solution.py:40
  46.9 16.8 %fusion.16 = bf16[4,192,2048]{2,1,0:T(8,128)(2,1)} fusion(bf16[256,4,8,2048]{3,2,1,0:T(8,128)(2,1)} %bitcast.242, f32[192,2048]{1,0:T(8,128)} %fusion.49, f32[192,2048]{1,0:T(8,128)} %shard_map.68), kind=kOutput, calls=%fused_computation.24 | convolution fusion | flops 6444810240 | bytes 39845888 | tf_op jit(solution)/shard_map/tc,cbd->btd/dot_general | solution.py:110
  63.7 15.9 %all-gather.3.cloned.1.call-done = bf16[768,2048]{1,0:T(8,128)(2,1)} async-done(((bf16[192,2048]{1,0:T(8,128)(2,1)}), bf16[768,2048]{1,0:T(8,128)(2,1)}) %all-gather.3.cloned.1.call-update) | async-done | bytes 3145744 | tf_op jit(solution)/shard_map/all_gather | solution.py:118
  79.6 19.2 %fusion.19 = f32[192,2048]{1,0:T(8,128)} fusion(bf16[4,192,2048]{2,1,0:T(8,128)(2,1)} %bitcast.244, bf16[256,4,8,2048]{3,2,1,0:T(8,128)(2,1)} %bitcast.243), kind=kOutput, calls=%fused_computation.25 | convolution fusion | flops 6442450944 | bytes 38273024 | tf_op jit(solution)/shard_map/bte,cbe->tc/dot_general | solution.py:119
  98.7 2.9 %fusion.64 = (f32[192,2048]{1,0:T(8,128)S(1)}, f32[192,2048]{1,0:T(8,128)S(1)}) fusion(f32[192,2048]{1,0:T(8,128)} %fusion.19, f32[192,2048]{1,0:T(8,128)} %shard_map.68, f32[192,2048]{1,0:T(8,128)} %fusion.49), kind=kLoop, calls=%fused_computation.106 | loop fusion | flops 786432 | bytes 7864320 | tf_op jit(solution)/shard_map/mul | solution.py:123
  101.7 1.3 collective-permute-start.4
  103.2 1.5 %collective-permute-start.3 = (f32[6,2048]{1,0:T(8,128)S(1)}, f32[6,2048]{1,0:T(8,128)S(1)}, u32[]{:S(2)}, u32[]{:S(2)}) collective-permute-start(f32[6,2048]{1,0:T(8,128)S(1)} %slice.379), channel_id=1, source_target_pairs={{4,0},{8,4},{12,8},{16,12},{20,16},{24,20},{28,24},{5,1},{9,5},{13... | collective-permute-start | bytes 147464 | tf_op jit(solution)/shard_map/ppermute | solution.py:124
  104.7 0.7 pad_convert_fusion.base_ref
  105.5 1.5 collective-permute-done.3
  107.0 1.3 maximum_bitcast_fusion
  108.3 1.9 %maximum_maximum_fusion.1.ext_ref = f32[384,2048]{1,0:T(8,128)} fusion(f32[133,2048]{1,0:T(8,128)S(1)} %collective-permute-done.4, f32[192,2048]{1,0:T(8,128)S(1)} %get-tuple-element.18, f32[384]{0:T(512)S(1)} %pad.16.clone), kind=kLoop, calls=%fused_computation.23 | loop fusion | flops 1572864 | bytes 5809664 | tf_op jit(solution)/shard_map/concatenate | solution.py:125
  110.2 13.3 %shard_map.69 = f32[224,2048]{1,0:T(8,128)} custom-call(f32[128,256]{1,0:T(8,128)} %pad_convert_fusion.base_ref, f32[384,2048]{1,0:T(8,128)} %maximum_maximum_fusion.1.ext_ref), custom_call_target="tpu_custom_call" | custom-call | flops 3758096384 | bytes 5111808 | tf_op jit(solution)/shard_map/pallas_call | solution.py:40
  123.6 2.0 %multiply_bitcast_fusion.1 = (f32[198,1,2048]{2,0,1:T(8,128)S(1)}, f32[198,1,2048]{2,0,1:T(8,128)S(1)}) fusion(f32[198,2048]{1,0:T(8,128)S(1)} %fusion.23, f32[224,2048]{1,0:T(8,128)} %shard_map.69, f32[198,2048]{1,0:T(8,128)S(1)} %fusion.36), kind=kLoop, calls=%fused_computation.69 | loop fusion | flops 811008 | bytes 8110080 | tf_op jit(solution)/shard_map/stack | solution.py:130
  125.5 0.6 pad_maximum_fusion
  126.2 5.0 %fusion.7 = bf16[192,3,2048]{2,0,1:T(8,128)(2,1)} fusion(f32[198,3,2048]{2,0,1:T(8,128)S(1)} %pad_maximum_fusion, f32[3,2048]{1,0:T(4,128)S(1)} %get-tuple-element.47, f32[3,2048]{1,0:T(4,128)S(1)} %get-tuple-element.48, f32[3,2048]{1,0:T(4,128)S(1)} %get-tuple-element.49, f32[3,2048]{1,0:T(4,128)S(1)} %get-tuple-element.50, ...), kind=kLoop, calls=%fused_computation.9 | loop fusion | flops 16515072 | bytes 35561472 | tf_op jit(solution)/shard_map/convert_element_type | solution.py:134
  131.1 10.4 %reduce-scatter.2.cloned.1.call-done = bf16[1,192,2048]{2,1,0:T(8,128)(2,1)} async-done(((bf16[4,192,2048]{2,1,0:T(8,128)(2,1)}), bf16[1,192,2048]{2,1,0:T(8,128)(2,1)}) %reduce-scatter.2.cloned.1.call-update) | async-done | bytes 786448 | tf_op jit(solution)/shard_map/reduce_scatter | solution.py:113
  (36 shorter events, 0.6 us)
Async XLA Ops:
  7.2 9.6 %copy-start.1 = (f32[7,3,2048]{2,0,1:T(8,128)S(1)}, f32[7,3,2048]{2,0,1:T(8,128)}, u32[]{:S(2)}) copy-start(f32[7,3,2048]{2,0,1:T(8,128)} %param.6) | copy-start | bytes 516100
  7.2 72.4 %all-gather.3.cloned.1.call-start = ((), (), s32[]{:S(2)}) async-start(), calls=%async_computation.2 | async-start | bytes 3932160 | tf_op jit(solution)/shard_map/all_gather | solution.py:118
  8.2 10.1 %collective-permute-start.1 = (bf16[6,3,2048]{2,0,1:T(8,128)(2,1)S(1)}, bf16[6,3,2048]{2,0,1:T(8,128)(2,1)S(1)}, u32[]{:S(2)}, u32[]{:S(2)}) collective-permute-start(bf16[6,3,2048]{2,0,1:T(8,128)(2,1)S(1)} %get-tuple-element.14), channel_id=1, source_target_pairs={{4,0},{8,4},{12,8},{16,12},{20,16},{24,20},{28,24},{5,1},{9,5},{13... | collective-permute-start | bytes 221192 | tf_op jit(solution)/shard_map/ppermute | solution.py:84
  9.5 8.8 %collective-permute-start = (bf16[6,3,2048]{2,0,1:T(8,128)(2,1)S(1)}, bf16[6,3,2048]{2,0,1:T(8,128)(2,1)S(1)}, u32[]{:S(2)}, u32[]{:S(2)}) collective-permute-start(bf16[6,3,2048]{2,0,1:T(8,128)(2,1)S(1)} %get-tuple-element.13), channel_id=1, source_target_pairs={{0,4},{4,8},{8,12},{12,16},{16,20},{20,24},{24,28},{1,5},{5,9},{9,... | collective-permute-start | bytes 221192 | tf_op jit(solution)/shard_map/ppermute | solution.py:83
  12.6 128.9 %reduce-scatter.2.cloned.1.call-start = ((), (), s32[]{:S(2)}) async-start(), calls=%async_computation.1 | async-start | bytes 3932160 | tf_op jit(solution)/shard_map/reduce_scatter | solution.py:113
  24.4 7.2 %collective-permute-start.2 = (f32[127,2048]{1,0:T(8,128)S(1)}, f32[127,2048]{1,0:T(8,128)S(1)}, u32[]{:S(2)}, u32[]{:S(2)}) collective-permute-start(f32[127,2048]{1,0:T(8,128)S(1)} %slice.378), channel_id=1, source_target_pairs={{0,4},{4,8},{8,12},{12,16},{16,20},{20,24},{24,28},{1,5},{5,9},{9,... | collective-permute-start | bytes 3121160 | tf_op jit(solution)/shard_map/ppermute | solution.py:101
  101.6 1.4 copy-start.6
  101.6 1.4 copy-start.7
  101.6 1.5 copy-start.4
  101.6 1.5 copy-start.5
  101.6 3.0 %copy-start.2 = (bf16[128,128]{1,0:T(8,128)(2,1)S(1)}, bf16[128,128]{1,0:T(8,128)(2,1)}, u32[]{:S(2)}) copy-start(bf16[128,128]{1,0:T(8,128)(2,1)} %convert.9) | copy-start | bytes 98308
  101.7 3.8 %copy-start.3 = (f32[1,3,2048]{2,0,1:T(1,128)S(1)}, f32[1,3,2048]{2,0,1:T(1,128)}, u32[]{:S(2)}) copy-start(f32[1,3,2048]{2,0,1:T(1,128)} %get-tuple-element.19) | copy-start | bytes 73732
  101.7 6.5 %collective-permute-start.4 = (f32[133,2048]{1,0:T(8,128)S(1)}, f32[133,2048]{1,0:T(8,128)S(1)}, u32[]{:S(2)}, u32[]{:S(2)}) collective-permute-start(f32[133,2048]{1,0:T(8,128)S(1)} %slice.380), channel_id=1, source_target_pairs={{4,0},{8,4},{12,8},{16,12},{20,16},{24,20},{28,24},{5,1},{9,5},{13... | collective-permute-start | bytes 3268616 | tf_op jit(solution)/shard_map/ppermute | solution.py:124
  103.2 3.8 %collective-permute-start.3 = (f32[6,2048]{1,0:T(8,128)S(1)}, f32[6,2048]{1,0:T(8,128)S(1)}, u32[]{:S(2)}, u32[]{:S(2)}) collective-permute-start(f32[6,2048]{1,0:T(8,128)S(1)} %slice.379), channel_id=1, source_target_pairs={{4,0},{8,4},{12,8},{16,12},{20,16},{24,20},{28,24},{5,1},{9,5},{13... | collective-permute-start | bytes 147464 | tf_op jit(solution)/shard_map/ppermute | solution.py:124
  123.6 2.0 %copy-start = (f32[198,1,2048]{2,0,1:T(8,128)S(1)}, f32[198,1,2048]{2,0,1:T(8,128)}, u32[]{:S(2)}) copy-start(f32[198,1,2048]{2,0,1:T(8,128)} %maximum_bitcast_fusion) | copy-start | bytes 4866052
Sparse Core Ops, SparseCore 0:
  12.7 66.8 all-gather.2
  82.4 59.0 reduce-scatter.1

commit v6 on v4

--- a/solution.py
+++ b/solution.py
@@ -8,12 +8,18 @@
 LANES = 128
 
 
-def _toeplitz_kernel(base_ref, ext_ref, out_ref):
+def _toeplitz_kernel(*refs):
+    base_ref, *part_refs, out_ref = refs
     gb, span = base_ref.shape
     rows, width = out_ref.shape
     half = rows // 2
     hg = width // gb
-    p = ext_ref[...]
+    pieces = [r[...] for r in part_refs]
+    filled = sum(x.shape[0] for x in pieces)
+    need = half + span
+    if filled < need:
+        pieces.append(jnp.zeros((need - filled, width), jnp.float32))
+    p = jnp.concatenate(pieces, axis=0)
     p2 = jnp.concatenate([p[:span], p[half:half + span]], axis=1)
     p_hi = p2.astype(jnp.bfloat16)
     p_lo = (p2 - p_hi.astype(jnp.float32)).astype(jnp.bfloat16)
@@ -29,27 +35,27 @@
     out_ref[pl.ds(half, half), :] = acc[:, width:]
 
 
-def toeplitz_conv(base, ext, rows):
+def toeplitz_conv(base, parts, rows):
     groups, span = base.shape
-    length, channels = ext.shape
+    channels = parts[0].shape[1]
     half = rows // 2
-    assert rows % 32 == 0 and half + span <= length and span >= half + LANES - 1
+    assert rows % 32 == 0 and all(x.shape[0] % 8 == 0 for x in parts)
+    assert sum(x.shape[0] for x in parts) <= half + span
     gb = groups * LANES // channels
     steps = channels // LANES
     flops = 4 * half * span * 2 * LANES * gb * steps
+    in_specs = [pl.BlockSpec((gb, span), lambda i: (i, 0))]
+    in_specs += [pl.BlockSpec((x.shape[0], LANES), lambda i: (0, i)) for x in parts]
     return pl.pallas_call(
         _toeplitz_kernel,
         grid=(steps,),
-        in_specs=[
-            pl.BlockSpec((gb, span), lambda i: (i, 0)),
-            pl.BlockSpec((length, LANES), lambda i: (0, i)),
-        ],
+        in_specs=in_specs,
         out_specs=pl.BlockSpec((rows, LANES), lambda i: (0, i)),
         out_shape=jax.ShapeDtypeStruct((rows, channels), jnp.float32),
         cost_estimate=pl.CostEstimate(
             flops=flops, transcendentals=0,
-            bytes_accessed=4 * (base.size + ext.size + rows * channels)),
-    )(base, ext)
+            bytes_accessed=4 * (base.size + sum(x.size for x in parts) + rows * channels)),
+    )(base, *parts)
 
 
 def shift_perm(n, step):
@@ -62,7 +68,6 @@
     rows = projected.shape[0]
     feat_len = feat_taps.shape[0]
     filt_len = filters.shape[1]
-    channels = projected.shape[2]
     n = lax.axis_size("seq")
     fwd = shift_perm(n, 1)
     bwd = shift_perm(n, -1)
@@ -70,12 +75,13 @@
     lh = filt_len - 1
     reach = lh + fh
     assert reach <= rows
-    ext_len = -(-(rows + reach) // LANES) * LANES
     fwd_rows = rows
     bwd_rows = -(-(rows + fh) // 32) * 32
-    span_f = -(-(fwd_rows // 2 + lh) // LANES) * LANES
+    span_f = -(-(fwd_rows // 2 + filt_len) // LANES) * LANES
+    halo_f = -(-filt_len // 8) * 8
+    halo_b = -(-reach // 8) * 8
     span_b = -(-(bwd_rows // 2 + lh) // LANES) * LANES
-    base_fwd = jnp.pad(filters[:, ::-1], ((0, 0), (0, span_f - filt_len))).astype(jnp.bfloat16)
+    base_fwd = jnp.pad(filters[:, ::-1], ((0, 0), (halo_f - filt_len + 1, span_f - halo_f - 1))).astype(jnp.bfloat16)
     base_bwd = jnp.pad(filters, ((0, 0), (0, span_b - filt_len))).astype(jnp.bfloat16)
     base_fwd = base_fwd.astype(jnp.float32)
     base_bwd = base_bwd.astype(jnp.float32)
@@ -98,11 +104,8 @@
     value_feat = value_ext[:rows]
     product = key_feat * value_feat
 
-    prev_prod = lax.ppermute(product[rows - lh:], "seq", fwd)
-    pext = jnp.concatenate(
-        [prev_prod, product, jnp.zeros((ext_len - rows - lh, channels), jnp.float32)], axis=0
-    )
-    conv = toeplitz_conv(base_fwd, pext, fwd_rows)
+    prev_prod = lax.ppermute(product[rows - halo_f:], "seq", fwd)
+    conv = toeplitz_conv(base_fwd, [prev_prod, product], fwd_rows)
     mixed = (query * conv).astype(jnp.bfloat16)
 
     partial = jnp.einsum(
@@ -119,11 +122,8 @@
     )
     signal_grad = grad_mixed * query
     query_grad = grad_mixed * conv
-    next_sig, next_qg = lax.ppermute((signal_grad[:reach], query_grad[:fh]), "seq", bwd)
-    sext = jnp.concatenate(
-        [signal_grad, next_sig, jnp.zeros((ext_len - rows - reach, channels), jnp.float32)], axis=0
-    )
-    conv_grad = toeplitz_conv(base_bwd, sext, bwd_rows)[:rows + fh]
+    next_sig, next_qg = lax.ppermute((signal_grad[:halo_b], query_grad[:fh]), "seq", bwd)
+    conv_grad = toeplitz_conv(base_bwd, [signal_grad, next_sig], bwd_rows)[:rows + fh]
     qg_ext = jnp.concatenate([query_grad, next_qg], axis=0)
     dext = jnp.stack([qg_ext, conv_grad * value_ext, conv_grad * key_ext], axis=1)
     igrad = feat_taps[0] * dext[:rows]

time: 150 us -> 150 us (level)
  other arithmetic: 25.6 us -> 20.3 us
  local copies, waits for them, and re-layouts: 4.91 us -> 8.86 us
    concatenate x2 -> x0, other arithmetic: 3.89 us -> none  [the longest x1 1.96 us: block(): jnp.concatenate([prev_prod, product, jnp.zeros((ext_len - rows - lh, chan...]
    slice x2, local copies, waits for them, and re-layouts: 1.76 us -> 3.88 us  [featurize(): out = feat_taps[0, stream] * sig[fh:fh + out_rows]]
    reduce_scatter x1, waiting for transfers between devices: 12.5 us -> 14.5 us  [block(): output = lax.psum_scatter(partial, 'tp', scatter_dimension=1, tiled=True)]
    all_gather x1, waiting for transfers between devices: 15.8 us -> 14.1 us  [block(): cot_full = lax.all_gather(cotangent, 'tp', axis=1, tiled=True)]
    slice x1, local copies, waits for them, and re-layouts: 0.77 us -> 2.45 us  [block(): igrad = feat_taps[0] * dext[:rows]]
  transfers between devices with their start and end apart: 7 -> 7, of which waited for: 3 -> 3; matrix products, arithmetic and copies ran while one was open for 43% -> 42% of each run, Pallas kernels for 18% -> 18%
where the time goes in v6:
time: 150 us; the launch traced here: 148 us
  matrix products  34.9 us (23%)
  waiting for transfers between devices  30.5 us (20%)
  Pallas kernels  26.8 us (18%)
  other arithmetic  20.3 us (14%)
  between operations  14.3 us (10%)
  starting transfers between devices  12.6 us (8%)
  local copies, waits for them, and re-layouts  8.86 us (6%)
    pallas_call x2, Pallas kernels, toeplitz_conv(): pl.pallas_call(_toeplitz_kernel, grid=(steps,), in_specs=in_specs, out_sp...  26.8 us
    dot_general x1, matrix products, block(): jnp.einsum('te,ce->tc', cot_full, out_weight, preferred_element_type=jnp....  18.2 us
    dot_general x1, matrix products, block(): jnp.einsum('tc,cd->td', mixed, out_weight, preferred_element_type=jnp.flo...  16.7 us
    reduce_scatter x1, waiting for transfers between devices, block(): output = lax.psum_scatter(partial, 'tp', scatter_dimension=1, tiled=True)  14.5 us
    all_gather x1, waiting for transfers between devices, block(): cot_full = lax.all_gather(cotangent, 'tp', axis=1, tiled=True)  14.1 us
    ppermute x1, starting transfers between devices, block(): prev_prod = lax.ppermute(product[rows - halo_f:], 'seq', fwd)  5.64 us
    add x3, other arithmetic, featurize(): out = out + feat_taps[d, stream] * sig[fh - d:fh - d + out_rows]  5.08 us
    convert_element_type x1, other arithmetic, block(): return (output, igrad.astype(jnp.bfloat16))  4.96 us
  transfers between devices with their start and end apart: 7, of which 3 were waited for; matrix products, arithmetic and copies ran while one was open for 42% of the time, Pallas kernels for 18%

profile of v6, /device:TPU:0, one launch (start us, length us, event | category | flops | bytes accessed | tf_op | source)
XLA Modules:
  0.0 148.3 jit_solution(13119683600729754516)
XLA Ops:
  7.2 1.0 fusion.46
  8.2 1.3 collective-permute-start.1
  9.5 3.0 %collective-permute-start = (bf16[6,3,2048]{2,0,1:T(8,128)(2,1)S(1)}, bf16[6,3,2048]{2,0,1:T(8,128)(2,1)S(1)}, u32[]{:S(2)}, u32[]{:S(2)}) collective-permute-start(bf16[6,3,2048]{2,0,1:T(8,128)(2,1)S(1)} %get-tuple-element.13), channel_id=1, source_target_pairs={{0,4},{4,8},{8,12},{12,16},{16,20},{20,24},{24,28},{1,5},{5,9},{9,... | collective-permute-start | bytes 221192 | tf_op jit(solution)/shard_map/ppermute | solution.py:89
  12.6 2.4 %fusion.49 = (f32[1,1,2048]{2,0,1:T(1,128)S(1)}, f32[1,1,2048]{2,0,1:T(1,128)S(1)}, f32[1,1,2048]{2,0,1:T(1,128)S(1)}, f32[1,1,2048]{2,0,1:T(1,128)S(1)}, f32[1,...) fusion(f32[7,3,2048]{2,0,1:T(8,128)} %param.6), kind=kLoop, calls=%fused_computation.97 | loop fusion | bytes 311296 | tf_op jit(solution)/shard_map/slice | solution.py:95
  15.0 2.4 %fusion.48 = (f32[1,3,2048]{2,0,1:T(1,128)S(1)}, f32[1,3,2048]{2,0,1:T(1,128)S(1)}, f32[1,3,2048]{2,0,1:T(1,128)S(1)}, f32[1,3,2048]{2,0,1:T(1,128)S(1)}, f32[1,...) fusion(f32[7,3,2048]{2,0,1:T(8,128)} %param.6), kind=kLoop, calls=%fused_computation.96 | loop fusion | bytes 344064 | tf_op jit(solution)/shard_map/slice | solution.py:129
  17.4 1.5 %fusion.50 = (f32[1,1,2048]{2,0,1:T(1,128)}, f32[1,1,2048]{2,0,1:T(1,128)}) fusion(f32[7,3,2048]{2,0,1:T(8,128)} %param.6), kind=kLoop, calls=%fused_computation.98 | loop fusion | bytes 32768 | tf_op jit(solution)/shard_map/slice | solution.py:95
  18.9 0.1 rev.3
  19.0 2.4 %pad_maximum_fusion.1 = bf16[204,3,2048]{2,0,1:T(8,128)(2,1)S(1)} fusion(bf16[6,3,2048]{2,0,1:T(8,128)(2,1)S(1)} %collective-permute-done.1, bf16[192,3,2048]{2,0,1:T(8,128)(2,1)} %param.5, bf16[6,3,2048]{2,0,1:T(8,128)(2,1)S(1)} %collective-permute-done), kind=kLoop, calls=%fused_computation.16 | loop fusion | flops 7520256 | bytes 5013504 | tf_op jit(solution)/shard_map/concatenate | solution.py:91
  21.5 0.7 slice_convert_fusion.1
  22.2 1.3 fusion.8
  23.6 1.3 fusion.21
  24.9 0.2 slice_multiply_fusion.7.refs_2_
  25.1 1.2 copy-done.3
  26.4 5.6 %collective-permute-start.2 = (f32[128,2048]{1,0:T(8,128)S(1)}, f32[128,2048]{1,0:T(8,128)}, u32[]{:S(2)}, u32[]{:S(2)}) collective-permute-start(f32[128,2048]{1,0:T(8,128)S(1)} %slice.378), channel_id=1, source_target_pairs={{0,4},{4,8},{8,12},{12,16},{16,20},{20,24},{24,28},{1,5},{5,9},{9,... | collective-permute-start | bytes 3145736 | tf_op jit(solution)/shard_map/ppermute | solution.py:107
  32.0 0.7 pad_convert_fusion.1.refs_0_
  32.8 2.4 %fusion.34 = f32[192,2048]{1,0:T(8,128)} fusion(f32[204,1,2048]{2,0,1:T(8,128)S(1)} %get-tuple-element.12, f32[2048]{0:T(1024)S(1)} %bitcast.202, f32[2048]{0:T(1024)S(1)} %bitcast.203, f32[2048]{0:T(1024)S(1)} %bitcast.204, f32[2048]{0:T(1024)S(1)} %bitcast.205, f32[2048]{0:T(1024)S(1)} %bitcast.206, f32[2048]{0:T(1024)S(1)} %bitcast.222, f32[2048]{0:T(1024)S(1)} %bitcast.221), kind=kLoop, calls=%fused_computation.63 | loop fusion | flops 5111808 | bytes 12640256 | tf_op jit(solution)/shard_map/add | solution.py:97
  35.2 13.4 %shard_map.68 = f32[192,2048]{1,0:T(8,128)} custom-call(f32[128,256]{1,0:T(8,128)} %pad_convert_fusion.1.refs_0_, f32[128,2048]{1,0:T(8,128)} %collective-permute-done.2.refs_1_, f32[192,2048]{1,0:T(8,128)} %copy-done.3), custom_call_target="tpu_custom_call" | custom-call | flops 3221225472 | bytes 4325376 | tf_op jit(solution)/shard_map/pallas_call | solution.py:49
  48.7 16.7 %convolution_convert_fusion = bf16[192,8192]{1,0:T(8,128)(2,1)} fusion(bf16[2048,8192]{1,0:T(8,128)(2,1)} %param.8, f32[192,2048]{1,0:T(8,128)} %fusion.34, f32[192,2048]{1,0:T(8,128)} %shard_map.68), kind=kOutput, calls=%fused_computation | convolution fusion | flops 6444810240 | bytes 39845888 | tf_op jit(solution)/shard_map/tc,cd->td/dot_general | solution.py:111
  65.4 14.1 %all-gather.2.cloned.1.call-done = bf16[192,8192]{1,0:T(8,128)(2,1)} async-done(((bf16[192,2048]{1,0:T(8,128)(2,1)}), bf16[192,8192]{1,0:T(8,128)(2,1)}) %all-gather.2.cloned.1.call-update) | async-done | bytes 3145744 | tf_op jit(solution)/shard_map/all_gather | solution.py:119
  79.5 18.2 %fusion.51 = f32[192,2048]{1,0:T(8,128)} fusion(bf16[192,8192]{1,0:T(8,128)(2,1)} %all-gather.2.cloned.1.call-done, bf16[2048,8192]{1,0:T(8,128)(2,1)} %param.8), kind=kOutput, calls=%fused_computation.99 | convolution fusion | flops 6442450944 | bytes 38273024 | tf_op jit(solution)/shard_map/te,ce->tc/dot_general | solution.py:120
  97.7 1.7 %fusion.47 = (f32[192,2048]{1,0:T(8,128)S(1)}, f32[192,2048]{1,0:T(8,128)S(1)}) fusion(f32[192,2048]{1,0:T(8,128)} %fusion.51, f32[192,2048]{1,0:T(8,128)S(1)} %copy-done.4, f32[192,2048]{1,0:T(8,128)S(1)} %copy-done.1), kind=kLoop, calls=%fused_computation.95 | loop fusion | flops 786432 | bytes 7864320 | tf_op jit(solution)/shard_map/mul | solution.py:124
  99.5 0.1 slice.380
  99.5 1.3 collective-permute-start.4
  100.9 1.3 collective-permute-start.3
  102.2 0.7 pad_convert_fusion.refs_0_
  102.9 1.8 %collective-permute-done.3 = f32[6,2048]{1,0:T(8,128)S(1)} collective-permute-done((f32[6,2048]{1,0:T(8,128)S(1)}, f32[6,2048]{1,0:T(8,128)S(1)}, u32[]{:S(2)}, u32[]{:S(2)}) %collective-permute-start.3) | collective-permute-done | bytes 49184 | tf_op jit(solution)/shard_map/ppermute | solution.py:125
  104.7 1.4 maximum_bitcast_fusion
  106.1 13.4 %shard_map.69 = f32[224,2048]{1,0:T(8,128)} custom-call(f32[128,256]{1,0:T(8,128)} %pad_convert_fusion.refs_0_, f32[192,2048]{1,0:T(8,128)} %copy-done.2, f32[136,2048]{1,0:T(8,128)} %collective-permute-done.4.refs_2_), custom_call_target="tpu_custom_call" | custom-call | flops 3758096384 | bytes 4653056 | tf_op jit(solution)/shard_map/pallas_call | solution.py:49
  119.5 1.9 %multiply_bitcast_fusion.1 = (f32[198,1,2048]{2,0,1:T(8,128)S(1)}, f32[198,1,2048]{2,0,1:T(8,128)S(1)}) fusion(f32[198,2048]{1,0:T(8,128)S(1)} %fusion.8, f32[224,2048]{1,0:T(8,128)} %shard_map.69, f32[198,2048]{1,0:T(8,128)S(1)} %fusion.21), kind=kLoop, calls=%fused_computation.59 | loop fusion | flops 811008 | bytes 8110080 | tf_op jit(solution)/shard_map/stack | solution.py:128
  121.4 0.6 pad_maximum_fusion
  122.0 5.0 %fusion.1 = bf16[192,3,2048]{2,0,1:T(8,128)(2,1)} fusion(f32[198,3,2048]{2,0,1:T(8,128)S(1)} %pad_maximum_fusion, f32[3,2048]{1,0:T(4,128)S(1)} %get-tuple-element.47, f32[3,2048]{1,0:T(4,128)S(1)} %get-tuple-element.48, f32[3,2048]{1,0:T(4,128)S(1)} %get-tuple-element.49, f32[3,2048]{1,0:T(4,128)S(1)} %get-tuple-element.50, ...), kind=kLoop, calls=%fused_computation.4 | loop fusion | flops 16515072 | bytes 35561472 | tf_op jit(solution)/shard_map/convert_element_type | solution.py:132
  127.0 14.5 %reduce-scatter.2.cloned.1.call-done = bf16[192,2048]{1,0:T(8,128)(2,1)} async-done(((bf16[192,8192]{1,0:T(8,128)(2,1)}), bf16[192,2048]{1,0:T(8,128)(2,1)}) %reduce-scatter.2.cloned.1.call-update) | async-done | bytes 786448 | tf_op jit(solution)/shard_map/reduce_scatter | solution.py:114
  (44 shorter events, 0.4 us)
Async XLA Ops:
  7.2 11.8 %copy-start.5 = (f32[128,128]{1,0:T(8,128)S(1)}, f32[128,128]{1,0:T(8,128)}, u32[]{:S(2)}) copy-start(f32[128,128]{1,0:T(8,128)} %param.7) | copy-start | bytes 196612
  7.2 72.4 %all-gather.2.cloned.1.call-start = ((), (), s32[]{:S(2)}) async-start(), calls=%async_computation.2 | async-start | bytes 3932160 | tf_op jit(solution)/shard_map/all_gather | solution.py:119
  8.2 10.8 %collective-permute-start.1 = (bf16[6,3,2048]{2,0,1:T(8,128)(2,1)S(1)}, bf16[6,3,2048]{2,0,1:T(8,128)(2,1)S(1)}, u32[]{:S(2)}, u32[]{:S(2)}) collective-permute-start(bf16[6,3,2048]{2,0,1:T(8,128)(2,1)S(1)} %get-tuple-element.14), channel_id=1, source_target_pairs={{4,0},{8,4},{12,8},{16,12},{20,16},{24,20},{28,24},{5,1},{9,5},{13... | collective-permute-start | bytes 221192 | tf_op jit(solution)/shard_map/ppermute | solution.py:90
  9.5 9.5 %collective-permute-start = (bf16[6,3,2048]{2,0,1:T(8,128)(2,1)S(1)}, bf16[6,3,2048]{2,0,1:T(8,128)(2,1)S(1)}, u32[]{:S(2)}, u32[]{:S(2)}) collective-permute-start(bf16[6,3,2048]{2,0,1:T(8,128)(2,1)S(1)} %get-tuple-element.13), channel_id=1, source_target_pairs={{0,4},{4,8},{8,12},{12,16},{16,20},{20,24},{24,28},{1,5},{5,9},{9,... | collective-permute-start | bytes 221192 | tf_op jit(solution)/shard_map/ppermute | solution.py:89
  12.6 128.9 %reduce-scatter.2.cloned.1.call-start = ((), (), s32[]{:S(2)}) async-start(), calls=%async_computation.1 | async-start | bytes 3932160 | tf_op jit(solution)/shard_map/reduce_scatter | solution.py:114
  22.2 1.4 copy-start.10
  22.2 1.4 copy-start.11
  22.2 1.4 copy-start.12
  25.1 1.2 copy-start.3
  26.3 6.5 %copy-start.7 = (f32[1,3,2048]{2,0,1:T(1,128)S(1)}, f32[1,3,2048]{2,0,1:T(1,128)}, u32[]{:S(2)}) copy-start(f32[1,3,2048]{2,0,1:T(1,128)} %get-tuple-element.25) | copy-start | bytes 73732
  26.3 6.5 %copy-start.8 = (f32[1,1,2048]{2,0,1:T(1,128)S(1)}, f32[1,1,2048]{2,0,1:T(1,128)}, u32[]{:S(2)}) copy-start(f32[1,1,2048]{2,0,1:T(1,128)} %get-tuple-element.43) | copy-start | bytes 24580
  26.3 6.5 %copy-start.9 = (f32[1,1,2048]{2,0,1:T(1,128)S(1)}, f32[1,1,2048]{2,0,1:T(1,128)}, u32[]{:S(2)}) copy-start(f32[1,1,2048]{2,0,1:T(1,128)} %get-tuple-element.44) | copy-start | bytes 24580
  26.3 6.5 %copy-start.13 = (f32[1,1,2048]{2,0,1:T(1,128)S(1)}, f32[1,1,2048]{2,0,1:T(1,128)}, u32[]{:S(2)}) copy-start(f32[1,1,2048]{2,0,1:T(1,128)} %get-tuple-element.45) | copy-start | bytes 24580
  26.3 6.6 %copy-start.14 = (f32[1,1,2048]{2,0,1:T(1,128)S(1)}, f32[1,1,2048]{2,0,1:T(1,128)}, u32[]{:S(2)}) copy-start(f32[1,1,2048]{2,0,1:T(1,128)} %get-tuple-element.46) | copy-start | bytes 24580
  26.4 8.9 %collective-permute-start.2 = (f32[128,2048]{1,0:T(8,128)S(1)}, f32[128,2048]{1,0:T(8,128)}, u32[]{:S(2)}, u32[]{:S(2)}) collective-permute-start(f32[128,2048]{1,0:T(8,128)S(1)} %slice.378), channel_id=1, source_target_pairs={{0,4},{4,8},{8,12},{12,16},{16,20},{20,24},{24,28},{1,5},{5,9},{9,... | collective-permute-start | bytes 3145736 | tf_op jit(solution)/shard_map/ppermute | solution.py:107
  79.5 18.2 %copy-start.1 = (f32[192,2048]{1,0:T(8,128)S(1)}, f32[192,2048]{1,0:T(8,128)}, u32[]{:S(2)}) copy-start(f32[192,2048]{1,0:T(8,128)} %fusion.34) | copy-start | bytes 4718596
  79.5 18.2 %copy-start.4 = (f32[192,2048]{1,0:T(8,128)S(1)}, f32[192,2048]{1,0:T(8,128)}, u32[]{:S(2)}) copy-start(f32[192,2048]{1,0:T(8,128)} %shard_map.68) | copy-start | bytes 4718596
  99.4 6.6 %copy-start.2 = (f32[192,2048]{1,0:T(8,128)}, f32[192,2048]{1,0:T(8,128)S(1)}, u32[]{:S(2)}) copy-start(f32[192,2048]{1,0:T(8,128)S(1)} %get-tuple-element.18.refs_1_) | copy-start | bytes 4718596
  99.4 1.4 copy-start.6
  99.5 6.5 %collective-permute-start.4 = (f32[136,2048]{1,0:T(8,128)S(1)}, f32[136,2048]{1,0:T(8,128)}, u32[]{:S(2)}, u32[]{:S(2)}) collective-permute-start(f32[136,2048]{1,0:T(8,128)S(1)} %slice.380), channel_id=1, source_target_pairs={{4,0},{8,4},{12,8},{16,12},{20,16},{24,20},{28,24},{5,1},{9,5},{13... | collective-permute-start | bytes 3342344 | tf_op jit(solution)/shard_map/ppermute | solution.py:125
  100.9 3.8 %collective-permute-start.3 = (f32[6,2048]{1,0:T(8,128)S(1)}, f32[6,2048]{1,0:T(8,128)S(1)}, u32[]{:S(2)}, u32[]{:S(2)}) collective-permute-start(f32[6,2048]{1,0:T(8,128)S(1)} %slice.379), channel_id=1, source_target_pairs={{4,0},{8,4},{12,8},{16,12},{20,16},{24,20},{28,24},{5,1},{9,5},{13... | collective-permute-start | bytes 147464 | tf_op jit(solution)/shard_map/ppermute | solution.py:125
  119.5 1.9 %copy-start = (f32[198,1,2048]{2,0,1:T(8,128)S(1)}, f32[198,1,2048]{2,0,1:T(8,128)}, u32[]{:S(2)}) copy-start(f32[198,1,2048]{2,0,1:T(8,128)} %maximum_bitcast_fusion) | copy-start | bytes 4866052
Sparse Core Ops, SparseCore 0:
  12.7 66.8 all-gather.1
  82.4 59.0 reduce-scatter.1

commit v7 on v4

--- a/solution.py
+++ b/solution.py
@@ -21,9 +21,12 @@
     acc = jnp.zeros((half, 2 * width), jnp.float32)
     for g in range(gb):
         t = jnp.broadcast_to(base_ref[pl.ds(g, 1), :], (half, span))
-        t = pltpu.roll(t, 0, 1, stride=1, stride_axis=0).astype(jnp.bfloat16)
-        res = jnp.dot(t, p_hi, preferred_element_type=jnp.float32)
-        res = res + jnp.dot(t, p_lo, preferred_element_type=jnp.float32)
+        t = pltpu.roll(t, 0, 1, stride=1, stride_axis=0)
+        t_hi = t.astype(jnp.bfloat16)
+        t_lo = (t - t_hi.astype(jnp.float32)).astype(jnp.bfloat16)
+        res = jnp.dot(t_hi, p_hi, preferred_element_type=jnp.float32)
+        res = res + jnp.dot(t_hi, p_lo, preferred_element_type=jnp.float32)
+        res = res + jnp.dot(t_lo, p_hi, preferred_element_type=jnp.float32)
         acc = jnp.where(lane_group == g, res, acc)
     out_ref[pl.ds(0, half), :] = acc[:, :width]
     out_ref[pl.ds(half, half), :] = acc[:, width:]
@@ -36,7 +39,7 @@
     assert rows % 32 == 0 and half + span <= length and span >= half + LANES - 1
     gb = groups * LANES // channels
     steps = channels // LANES
-    flops = 4 * half * span * 2 * LANES * gb * steps
+    flops = 6 * half * span * 2 * LANES * gb * steps
     return pl.pallas_call(
         _toeplitz_kernel,
         grid=(steps,),
@@ -75,10 +78,8 @@
     bwd_rows = -(-(rows + fh) // 32) * 32
     span_f = -(-(fwd_rows // 2 + lh) // LANES) * LANES
     span_b = -(-(bwd_rows // 2 + lh) // LANES) * LANES
-    base_fwd = jnp.pad(filters[:, ::-1], ((0, 0), (0, span_f - filt_len))).astype(jnp.bfloat16)
-    base_bwd = jnp.pad(filters, ((0, 0), (0, span_b - filt_len))).astype(jnp.bfloat16)
-    base_fwd = base_fwd.astype(jnp.float32)
-    base_bwd = base_bwd.astype(jnp.float32)
+    base_fwd = jnp.pad(filters[:, ::-1], ((0, 0), (0, span_f - filt_len)))
+    base_bwd = jnp.pad(filters, ((0, 0), (0, span_b - filt_len)))
 
     prev_proj = lax.ppermute(projected[rows - fh:], "seq", fwd)
     next_proj = lax.ppermute(projected[:fh], "seq", bwd)

time: 150 us -> 150 us (level)
  local copies, waits for them, and re-layouts: 4.91 us -> 7.99 us
  waiting for transfers between devices: 30.1 us -> 27.2 us
  other arithmetic: 25.6 us -> 22.8 us
  Pallas kernels: 26.8 us -> 29.4 us
    pallas_call x2, Pallas kernels: 26.8 us -> 29.4 us  [toeplitz_conv(): pl.pallas_call(_toeplitz_kernel, grid=(steps,), in_specs=[pl.BlockSpec((g...]
    slice x1, local copies, waits for them, and re-layouts: 0.77 us -> 2.45 us  [block(): igrad = feat_taps[0] * dext[:rows]]
    all_gather x1, waiting for transfers between devices: 15.8 us -> 14.2 us  [block(): cot_full = lax.all_gather(cotangent, 'tp', axis=1, tiled=True)]
  transfers between devices with their start and end apart: 7 -> 7, of which waited for: 3 -> 3; matrix products, arithmetic and copies ran while one was open for 43% -> 44% of each run, Pallas kernels for 18% -> 20%
where the time goes in v7:
time: 150 us; the launch traced here: 148 us
  matrix products  34.9 us (23%)
  Pallas kernels  29.4 us (20%)
  waiting for transfers between devices  27.2 us (18%)
  other arithmetic  22.8 us (15%)
  between operations  14.2 us (9%)
  starting transfers between devices  11.7 us (8%)
  local copies, waits for them, and re-layouts  7.99 us (5%)
    pallas_call x2, Pallas kernels, toeplitz_conv(): pl.pallas_call(_toeplitz_kernel, grid=(steps,), in_specs=[pl.BlockSpec((g...  29.4 us
    dot_general x1, matrix products, block(): jnp.einsum('te,ce->tc', cot_full, out_weight, preferred_element_type=jnp....  18.2 us
    dot_general x1, matrix products, block(): jnp.einsum('tc,cd->td', mixed, out_weight, preferred_element_type=jnp.flo...  16.7 us
    all_gather x1, waiting for transfers between devices, block(): cot_full = lax.all_gather(cotangent, 'tp', axis=1, tiled=True)  14.2 us
    reduce_scatter x1, waiting for transfers between devices, block(): output = lax.psum_scatter(partial, 'tp', scatter_dimension=1, tiled=True)  11.3 us
    add x3, other arithmetic, featurize(): out = out + feat_taps[d, stream] * sig[fh - d:fh - d + out_rows]  5.08 us
    convert_element_type x1, other arithmetic, block(): return (output, igrad.astype(jnp.bfloat16))  4.96 us
    ppermute x1, starting transfers between devices, block(): prev_prod = lax.ppermute(product[rows - lh:], 'seq', fwd)  4.73 us
  transfers between devices with their start and end apart: 7, of which 3 were waited for; matrix products, arithmetic and copies ran while one was open for 44% of the time, Pallas kernels for 20%

profile of v7, /device:TPU:0, one launch (start us, length us, event | category | flops | bytes accessed | tf_op | source)
XLA Modules:
  0.0 148.3 jit_solution(17454952394198196194)
XLA Ops:
  7.2 1.0 fusion.46
  8.2 1.3 collective-permute-start.1
  9.5 3.0 %collective-permute-start = (bf16[6,3,2048]{2,0,1:T(8,128)(2,1)S(1)}, bf16[6,3,2048]{2,0,1:T(8,128)(2,1)S(1)}, u32[]{:S(2)}, u32[]{:S(2)}) collective-permute-start(bf16[6,3,2048]{2,0,1:T(8,128)(2,1)S(1)} %get-tuple-element.13), channel_id=1, source_target_pairs={{0,4},{4,8},{8,12},{12,16},{16,20},{20,24},{24,28},{1,5},{5,9},{9,... | collective-permute-start | bytes 221192 | tf_op jit(solution)/shard_map/ppermute | solution.py:84
  12.6 1.7 %fusion.49 = (f32[1,1,2048]{2,0,1:T(1,128)S(1)}, f32[1,1,2048]{2,0,1:T(1,128)S(1)}, f32[1,1,2048]{2,0,1:T(1,128)S(1)}, f32[1,1,2048]{2,0,1:T(1,128)S(1)}, f32[1,...) fusion(f32[7,3,2048]{2,0,1:T(8,128)} %param.6), kind=kLoop, calls=%fused_computation.97 | loop fusion | bytes 311296 | tf_op jit(solution)/shard_map/slice | solution.py:90
  14.4 2.5 %fusion.48 = (f32[1,3,2048]{2,0,1:T(1,128)}, f32[1,3,2048]{2,0,1:T(1,128)S(1)}, f32[1,3,2048]{2,0,1:T(1,128)S(1)}, f32[1,3,2048]{2,0,1:T(1,128)}, f32[1,3,2048]{...) fusion(f32[7,3,2048]{2,0,1:T(8,128)} %param.6), kind=kLoop, calls=%fused_computation.96 | loop fusion | bytes 344064 | tf_op jit(solution)/shard_map/slice | solution.py:130
  16.9 0.7 pad.7.base_ref
  17.7 2.5 %pad_maximum_fusion.1 = bf16[204,3,2048]{2,0,1:T(8,128)(2,1)S(1)} fusion(bf16[6,3,2048]{2,0,1:T(8,128)(2,1)S(1)} %collective-permute-done.1, bf16[192,3,2048]{2,0,1:T(8,128)(2,1)} %param.5, bf16[6,3,2048]{2,0,1:T(8,128)(2,1)S(1)} %collective-permute-done), kind=kLoop, calls=%fused_computation.18 | loop fusion | flops 7520256 | bytes 5013504 | tf_op jit(solution)/shard_map/concatenate | solution.py:86
  20.2 0.7 slice_convert_fusion.1
  20.8 1.3 fusion.8
  22.2 1.3 fusion.21
  23.5 0.2 slice_multiply_fusion.7
  23.7 0.1 slice.378
  23.8 4.7 %collective-permute-start.2 = (f32[127,2048]{1,0:T(8,128)S(1)}, f32[127,2048]{1,0:T(8,128)S(1)}, u32[]{:S(2)}, u32[]{:S(2)}) collective-permute-start(f32[127,2048]{1,0:T(8,128)S(1)} %slice.378), channel_id=1, source_target_pairs={{0,4},{4,8},{8,12},{12,16},{16,20},{20,24},{24,28},{1,5},{5,9},{9,... | collective-permute-start | bytes 3121160 | tf_op jit(solution)/shard_map/ppermute | solution.py:102
  28.5 0.9 fusion.50
  29.4 2.4 %fusion.34 = f32[192,2048]{1,0:T(8,128)} fusion(f32[204,1,2048]{2,0,1:T(8,128)S(1)} %get-tuple-element.12, f32[2048]{0:T(1024)S(1)} %bitcast.202, f32[2048]{0:T(1024)S(1)} %bitcast.203, f32[2048]{0:T(1024)S(1)} %bitcast.204, f32[2048]{0:T(1024)S(1)} %bitcast.205, f32[2048]{0:T(1024)S(1)} %bitcast.206, f32[2048]{0:T(1024)S(1)} %bitcast.222, f32[2048]{0:T(1024)S(1)} %bitcast.221), kind=kLoop, calls=%fused_computation.65 | loop fusion | flops 5111808 | bytes 12640256 | tf_op jit(solution)/shard_map/add | solution.py:92
  31.9 1.9 %maximum_maximum_fusion.ext_ref = f32[384,2048]{1,0:T(8,128)} fusion(f32[192,2048]{1,0:T(8,128)S(1)} %slice_multiply_fusion.7, f32[127,2048]{1,0:T(8,128)S(1)} %collective-permute-done.2, f32[384]{0:T(512)S(1)} %pad.19.clone), kind=kLoop, calls=%fused_computation.16 | loop fusion | flops 1572864 | bytes 5760512 | tf_op jit(solution)/shard_map/concatenate | solution.py:103
  33.8 14.8 %shard_map.68 = f32[192,2048]{1,0:T(8,128)} custom-call(f32[128,256]{1,0:T(8,128)} %pad.7.base_ref, f32[384,2048]{1,0:T(8,128)} %maximum_maximum_fusion.ext_ref), custom_call_target="tpu_custom_call" | custom-call | flops 4831838208 | bytes 4849664 | tf_op jit(solution)/shard_map/pallas_call | solution.py:43
  48.6 16.7 %convolution_convert_fusion = bf16[192,8192]{1,0:T(8,128)(2,1)} fusion(bf16[2048,8192]{1,0:T(8,128)(2,1)} %param.8, f32[192,2048]{1,0:T(8,128)} %fusion.34, f32[192,2048]{1,0:T(8,128)} %shard_map.68), kind=kOutput, calls=%fused_computation | convolution fusion | flops 6444810240 | bytes 39845888 | tf_op jit(solution)/shard_map/tc,cd->td/dot_general | solution.py:109
  65.3 14.2 %all-gather.2.cloned.1.call-done = bf16[192,8192]{1,0:T(8,128)(2,1)} async-done(((bf16[192,2048]{1,0:T(8,128)(2,1)}), bf16[192,8192]{1,0:T(8,128)(2,1)}) %all-gather.2.cloned.1.call-update) | async-done | bytes 3145744 | tf_op jit(solution)/shard_map/all_gather | solution.py:117
  79.5 18.2 %fusion.51 = f32[192,2048]{1,0:T(8,128)} fusion(bf16[192,8192]{1,0:T(8,128)(2,1)} %all-gather.2.cloned.1.call-done, bf16[2048,8192]{1,0:T(8,128)(2,1)} %param.8), kind=kOutput, calls=%fused_computation.99 | convolution fusion | flops 6442450944 | bytes 38273024 | tf_op jit(solution)/shard_map/te,ce->tc/dot_general | solution.py:118
  97.7 1.7 %fusion.47 = (f32[192,2048]{1,0:T(8,128)S(1)}, f32[192,2048]{1,0:T(8,128)S(1)}) fusion(f32[192,2048]{1,0:T(8,128)} %fusion.51, f32[192,2048]{1,0:T(8,128)S(1)} %copy-done.2, f32[192,2048]{1,0:T(8,128)S(1)} %copy-done.1), kind=kLoop, calls=%fused_computation.95 | loop fusion | flops 786432 | bytes 7864320 | tf_op jit(solution)/shard_map/mul | solution.py:122
  99.6 1.3 collective-permute-start.4
  100.9 1.3 collective-permute-start.3
  102.3 0.7 pad.8.base_ref
  103.1 1.6 %collective-permute-done.3 = f32[6,2048]{1,0:T(8,128)S(1)} collective-permute-done((f32[6,2048]{1,0:T(8,128)S(1)}, f32[6,2048]{1,0:T(8,128)S(1)}, u32[]{:S(2)}, u32[]{:S(2)}) %collective-permute-start.3) | collective-permute-done | bytes 49184 | tf_op jit(solution)/shard_map/ppermute | solution.py:123
  104.7 1.3 maximum_bitcast_fusion
  106.0 1.9 %maximum_maximum_fusion.1.ext_ref = f32[384,2048]{1,0:T(8,128)} fusion(f32[133,2048]{1,0:T(8,128)S(1)} %collective-permute-done.4, f32[192,2048]{1,0:T(8,128)S(1)} %get-tuple-element.18, f32[384]{0:T(512)S(1)} %pad.14.clone), kind=kLoop, calls=%fused_computation.17 | loop fusion | flops 1572864 | bytes 5809664 | tf_op jit(solution)/shard_map/concatenate | solution.py:124
  108.0 14.6 %shard_map.69 = f32[224,2048]{1,0:T(8,128)} custom-call(f32[128,256]{1,0:T(8,128)} %pad.8.base_ref, f32[384,2048]{1,0:T(8,128)} %maximum_maximum_fusion.1.ext_ref), custom_call_target="tpu_custom_call" | custom-call | flops 5637144576 | bytes 5111808 | tf_op jit(solution)/shard_map/pallas_call | solution.py:43
  122.6 2.0 %multiply_bitcast_fusion.1 = (f32[198,1,2048]{2,0,1:T(8,128)S(1)}, f32[198,1,2048]{2,0,1:T(8,128)S(1)}) fusion(f32[198,2048]{1,0:T(8,128)S(1)} %fusion.8, f32[224,2048]{1,0:T(8,128)} %shard_map.69, f32[198,2048]{1,0:T(8,128)S(1)} %fusion.21), kind=kLoop, calls=%fused_computation.61 | loop fusion | flops 811008 | bytes 8110080 | tf_op jit(solution)/shard_map/stack | solution.py:129
  124.6 0.6 pad_maximum_fusion
  125.2 5.0 %fusion.1 = bf16[192,3,2048]{2,0,1:T(8,128)(2,1)} fusion(f32[198,3,2048]{2,0,1:T(8,128)S(1)} %pad_maximum_fusion, f32[3,2048]{1,0:T(4,128)S(1)} %get-tuple-element.47, f32[3,2048]{1,0:T(4,128)S(1)} %get-tuple-element.48, f32[3,2048]{1,0:T(4,128)S(1)} %get-tuple-element.49, f32[3,2048]{1,0:T(4,128)S(1)} %get-tuple-element.50, ...), kind=kLoop, calls=%fused_computation.4 | loop fusion | flops 16515072 | bytes 35561472 | tf_op jit(solution)/shard_map/convert_element_type | solution.py:133
  130.2 11.3 %reduce-scatter.2.cloned.1.call-done = bf16[192,2048]{1,0:T(8,128)(2,1)} async-done(((bf16[192,8192]{1,0:T(8,128)(2,1)}), bf16[192,2048]{1,0:T(8,128)(2,1)}) %reduce-scatter.2.cloned.1.call-update) | async-done | bytes 786448 | tf_op jit(solution)/shard_map/reduce_scatter | solution.py:112
  (33 shorter events, 0.6 us)
Async XLA Ops:
  7.2 9.7 %copy-start.3 = (f32[128,128]{1,0:T(8,128)S(1)}, f32[128,128]{1,0:T(8,128)}, u32[]{:S(2)}) copy-start(f32[128,128]{1,0:T(8,128)} %param.7) | copy-start | bytes 196612
  7.2 72.4 %all-gather.2.cloned.1.call-start = ((), (), s32[]{:S(2)}) async-start(), calls=%async_computation.2 | async-start | bytes 3932160 | tf_op jit(solution)/shard_map/all_gather | solution.py:117
  8.2 9.5 %collective-permute-start.1 = (bf16[6,3,2048]{2,0,1:T(8,128)(2,1)S(1)}, bf16[6,3,2048]{2,0,1:T(8,128)(2,1)S(1)}, u32[]{:S(2)}, u32[]{:S(2)}) collective-permute-start(bf16[6,3,2048]{2,0,1:T(8,128)(2,1)S(1)} %get-tuple-element.14), channel_id=1, source_target_pairs={{4,0},{8,4},{12,8},{16,12},{20,16},{24,20},{28,24},{5,1},{9,5},{13... | collective-permute-start | bytes 221192 | tf_op jit(solution)/shard_map/ppermute | solution.py:85
  9.5 8.2 %collective-permute-start = (bf16[6,3,2048]{2,0,1:T(8,128)(2,1)S(1)}, bf16[6,3,2048]{2,0,1:T(8,128)(2,1)S(1)}, u32[]{:S(2)}, u32[]{:S(2)}) collective-permute-start(bf16[6,3,2048]{2,0,1:T(8,128)(2,1)S(1)} %get-tuple-element.13), channel_id=1, source_target_pairs={{0,4},{4,8},{8,12},{12,16},{16,20},{20,24},{24,28},{1,5},{5,9},{9,... | collective-permute-start | bytes 221192 | tf_op jit(solution)/shard_map/ppermute | solution.py:84
  12.6 128.9 %reduce-scatter.2.cloned.1.call-start = ((), (), s32[]{:S(2)}) async-start(), calls=%async_computation.1 | async-start | bytes 3932160 | tf_op jit(solution)/shard_map/reduce_scatter | solution.py:112
  23.8 8.1 %collective-permute-start.2 = (f32[127,2048]{1,0:T(8,128)S(1)}, f32[127,2048]{1,0:T(8,128)S(1)}, u32[]{:S(2)}, u32[]{:S(2)}) collective-permute-start(f32[127,2048]{1,0:T(8,128)S(1)} %slice.378), channel_id=1, source_target_pairs={{0,4},{4,8},{8,12},{12,16},{16,20},{20,24},{24,28},{1,5},{5,9},{9,... | collective-permute-start | bytes 3121160 | tf_op jit(solution)/shard_map/ppermute | solution.py:102
  79.5 18.2 %copy-start.1 = (f32[192,2048]{1,0:T(8,128)S(1)}, f32[192,2048]{1,0:T(8,128)}, u32[]{:S(2)}) copy-start(f32[192,2048]{1,0:T(8,128)} %fusion.34) | copy-start | bytes 4718596
  79.5 18.2 %copy-start.2 = (f32[192,2048]{1,0:T(8,128)S(1)}, f32[192,2048]{1,0:T(8,128)}, u32[]{:S(2)}) copy-start(f32[192,2048]{1,0:T(8,128)} %shard_map.68) | copy-start | bytes 4718596
  99.5 2.8 %copy-start.5 = (f32[1,3,2048]{2,0,1:T(1,128)S(1)}, f32[1,3,2048]{2,0,1:T(1,128)}, u32[]{:S(2)}) copy-start(f32[1,3,2048]{2,0,1:T(1,128)} %get-tuple-element.22) | copy-start | bytes 73732
  99.5 2.8 %copy-start.6 = (f32[1,3,2048]{2,0,1:T(1,128)S(1)}, f32[1,3,2048]{2,0,1:T(1,128)}, u32[]{:S(2)}) copy-start(f32[1,3,2048]{2,0,1:T(1,128)} %get-tuple-element.23) | copy-start | bytes 73732
  99.5 3.6 %copy-start.4 = (f32[1,3,2048]{2,0,1:T(1,128)S(1)}, f32[1,3,2048]{2,0,1:T(1,128)}, u32[]{:S(2)}) copy-start(f32[1,3,2048]{2,0,1:T(1,128)} %get-tuple-element.19) | copy-start | bytes 73732
  99.6 6.5 %collective-permute-start.4 = (f32[133,2048]{1,0:T(8,128)S(1)}, f32[133,2048]{1,0:T(8,128)S(1)}, u32[]{:S(2)}, u32[]{:S(2)}) collective-permute-start(f32[133,2048]{1,0:T(8,128)S(1)} %slice.380), channel_id=1, source_target_pairs={{4,0},{8,4},{12,8},{16,12},{20,16},{24,20},{28,24},{5,1},{9,5},{13... | collective-permute-start | bytes 3268616 | tf_op jit(solution)/shard_map/ppermute | solution.py:123
  100.9 3.8 %collective-permute-start.3 = (f32[6,2048]{1,0:T(8,128)S(1)}, f32[6,2048]{1,0:T(8,128)S(1)}, u32[]{:S(2)}, u32[]{:S(2)}) collective-permute-start(f32[6,2048]{1,0:T(8,128)S(1)} %slice.379), channel_id=1, source_target_pairs={{4,0},{8,4},{12,8},{16,12},{20,16},{24,20},{28,24},{5,1},{9,5},{13... | collective-permute-start | bytes 147464 | tf_op jit(solution)/shard_map/ppermute | solution.py:123
  122.6 2.0 %copy-start = (f32[198,1,2048]{2,0,1:T(8,128)S(1)}, f32[198,1,2048]{2,0,1:T(8,128)}, u32[]{:S(2)}) copy-start(f32[198,1,2048]{2,0,1:T(8,128)} %maximum_bitcast_fusion) | copy-start | bytes 4866052
Sparse Core Ops, SparseCore 0:
  12.7 66.8 all-gather.1
  82.4 59.0 reduce-scatter.1
